TPU v7x, 32 devices: a whole 2x2x4 slice. The times are simulated.
32 devices in a mesh: chan: 8 (over y, x, core), win: 4 (over z).
Axes of the slice: x: 2, y: 2, z: 4, core: 2. Of those that a mesh axis runs over, the one named last changes fastest.
Arguments:
- record: bfloat16 [3, 1024, 32768], P(None, 'chan', 'win'), may hold values from -6 to 6
- chan_taps: float32 [33], replicated, may hold values from -1 to 1
- time_taps: float32 [65], replicated, may hold values from -0.75 to 0.75
- sources: int32 [3, 4], replicated, may hold values from 0 to 1023
Outputs:
- stacked: float32 [3, 4, 129, 1024], P(None, None, None, 'chan')
Inputs may be any that keep to these rules, and one draw needn't show every extreme that they name: `sources`: channel numbers of the fibre.
All inputs are finite; a program needn't handle non-finite values.
Results may differ from a plain program's by a relative error of at most 0.006.
Values may be sent and summed in bfloat16 or wider, within the bound.
No kernel may reach another device: no remote copies, remote signals or barrier semaphores. Data moves between devices by JAX's collectives and lax.ppermute only.
A program may use at most 128 MiB of HBM per device.

v0:
```python
import math

import jax
import jax.numpy as jnp
from jax import lax
from jax.sharding import PartitionSpec as P

LAG = 64


def padded_2(cells, sides, width):
    for axis, dim in sides:
        count = lax.axis_size(axis)
        ends = count - 1
        head = lax.slice_in_dim(cells, 0, width, axis=dim)
        tail = lax.slice_in_dim(cells, cells.shape[dim] - width, cells.shape[dim], axis=dim)
        cells = jnp.concatenate(
            [
                lax.ppermute(tail, axis, [(i, (i + 1) % count) for i in range(ends)]),
                cells,
                lax.ppermute(head, axis, [((i + 1) % count, i) for i in range(ends)]),
            ],
            axis=dim,
        )
    return cells


def tap_lookup(offset, tap_table):
    count_taps = tap_table.shape[0]
    marks = offset[..., None] == lax.iota(jnp.int32, count_taps)
    picked = jnp.where(marks, tap_table.astype(jnp.float32), jnp.zeros((), jnp.float32))
    return jnp.sum(picked, axis=-1).astype(tap_table.dtype)


def band_matrix(tap_table, height, breadth):
    offset = lax.iota(jnp.int32, breadth)[None, :] - lax.iota(jnp.int32, height)[:, None]
    return tap_lookup(offset, tap_table)


def time_filter(chan_pass, tap_table):
    channels_here, samples = chan_pass.shape
    half = (tap_table.shape[0] - 1) // 2
    blocks = chan_pass.reshape(channels_here, samples // 128, 128)
    zeros_block = jnp.zeros_like(blocks[:, :1])
    earlier = jnp.concatenate([zeros_block, blocks[:, :-1]], axis=1)
    later = jnp.concatenate([blocks[:, 1:], zeros_block], axis=1)
    extended = jnp.concatenate([earlier, blocks, later], axis=2)
    offset = lax.iota(jnp.int32, 384)[:, None] - 128 - lax.iota(jnp.int32, 128)[None, :] + half
    weights = tap_lookup(offset, tap_table)
    result = jnp.einsum("cbr,rt->cbt", extended, weights, preferred_element_type=jnp.float32)
    return result.reshape(channels_here, samples)


def whiten(time_pass):
    power = jnp.mean(time_pass * time_pass, axis=-1, keepdims=True)
    return (time_pass * lax.rsqrt(power + 1e-06)).astype(jnp.bfloat16)


def correlate(whitened, panel):
    samples = whitened.shape[1]
    padded = jnp.pad(panel, ((0, 0), (LAG, LAG)))
    shifted = jnp.stack(
        [padded[:, 2 * LAG - j : 2 * LAG - j + samples] for j in range(2 * LAG + 1)], axis=1
    )
    return jnp.einsum("cu,kju->kjc", whitened, shifted, preferred_element_type=jnp.float32)


def chan_filter(piece, tap_table):
    channels_here = piece.shape[0]
    half = (tap_table.shape[0] - 1) // 2
    widened = padded_2(piece, (("chan", 0),), half)
    total = jnp.dot(
        band_matrix(tap_table, channels_here, channels_here + 2 * half),
        widened,
        preferred_element_type=jnp.float32,
    )
    return total.astype(jnp.bfloat16)


def body(record, chan_taps, time_taps, sources):
    count_steps = record.shape[0]
    channels_here = record.shape[1]
    samples = record.shape[2]
    chan_table = chan_taps.astype(jnp.bfloat16)
    time_table = time_taps.astype(jnp.bfloat16)
    first_chan = lax.axis_index("chan") * channels_here
    selector = (
        (sources - first_chan)[:, :, None] == lax.iota(jnp.int32, channels_here)[None, None, :]
    ).astype(jnp.bfloat16)
    normalizer = 1.0 / math.sqrt(samples * lax.axis_size("win"))

    def prepare(section):
        return whiten(time_filter(chan_filter(record[section], chan_table), time_table))

    def local_panel(whitened, section):
        return jnp.dot(selector[section], whitened, preferred_element_type=jnp.float32)

    pairs = []
    prepared = [prepare(section) for section in range(count_steps)]
    terms = jnp.stack([local_panel(prepared[section], section) for section in range(count_steps)])
    panels = lax.psum(terms.astype(jnp.bfloat16), "chan")
    pairs = [(prepared[section], panels[section]) for section in range(count_steps)]
    partial_corr = [correlate(pair[0], pair[1]) for pair in pairs]
    summed = jnp.stack([lax.psum(term, "win") for term in partial_corr])
    return summed * normalizer


def solution(mesh):
    in_specs = (P(None, "chan", "win"), P(), P(), P())
    out_specs = P(None, None, None, "chan")
    return jax.shard_map(body, mesh=mesh, in_specs=in_specs, out_specs=out_specs, check_vma=False)
```

profile of v0, /device:TPU:0, one launch (start us, length us, event | category | flops | bytes accessed | tf_op | source)
XLA Modules:
  0.0 260.0 jit_solution(10230601745624962329)
XLA Ops:
  6.5 2.3 slice_bitcast_fusion.8
  8.8 3.1 %collective-permute-start = (bf16[16,8192]{1,0:T(8,128)(2,1)}, bf16[16,8192]{1,0:T(8,128)(2,1)}, u32[]{:S(2)}, u32[]{:S(2)}) collective-permute-start(bf16[16,8192]{1,0:T(8,128)(2,1)} %get-tuple-element.8), channel_id=1, source_target_pairs={{0,4},{4,8},{8,12},{12,16},{16,20},{20,24},{24,28},{1,5},{5,9},{9,... | collective-permute-start | bytes 786440 | tf_op jit(solution)/shard_map/ppermute | solution.py:19
  11.9 4.5 %collective-permute-start.4 = (bf16[16,8192]{1,0:T(8,128)(2,1)S(1)}, bf16[16,8192]{1,0:T(8,128)(2,1)}, u32[]{:S(2)}, u32[]{:S(2)}) collective-permute-start(bf16[16,8192]{1,0:T(8,128)(2,1)S(1)} %get-tuple-element.9), channel_id=1, source_target_pairs={{0,4},{4,8},{8,12},{12,16},{16,20},{20,24},{24,28},{1,5},{5,9},{9,... | collective-permute-start | bytes 786440 | tf_op jit(solution)/shard_map/ppermute | solution.py:19
  16.4 1.3 collective-permute-start.3
  17.7 3.8 %collective-permute-start.2 = (bf16[16,8192]{1,0:T(8,128)(2,1)S(1)}, bf16[16,8192]{1,0:T(8,128)(2,1)}, u32[]{:S(2)}, u32[]{:S(2)}) collective-permute-start(bf16[16,8192]{1,0:T(8,128)(2,1)S(1)} %get-tuple-element.11), channel_id=1, source_target_pairs={{0,4},{4,8},{8,12},{12,16},{16,20},{20,24},{24,28},{1,5},{5,9},{9,... | collective-permute-start | bytes 786440 | tf_op jit(solution)/shard_map/ppermute | solution.py:19
  21.5 1.3 collective-permute-start.1
  22.8 5.4 %slice_bitcast_fusion.2 = (bf16[128,8192]{1,0:T(8,128)(2,1)}, bf16[128,8192]{1,0:T(8,128)(2,1)S(1)}, bf16[128,8192]{1,0:T(8,128)(2,1)}) fusion(bf16[3,128,8192]{2,1,0:T(8,128)(2,1)} %param.4), kind=kLoop, calls=%fused_computation.89 | loop fusion | bytes 12582912 | tf_op jit(solution)/shard_map/squeeze | solution.py:93
  28.4 1.4 select_reduce_fusion
  30.2 1.5 collective-permute-start.5
  31.8 2.4 fusion.72
  34.9 1.7 fusion.78
  37.2 1.8 fusion.75
  39.5 1.5 fusion.121
  41.0 2.6 %multiply_reduce_fusion.1 = (f32[128]{0:T(128)S(1)}, f32[128,64,128]{0,2,1:T(8,128)S(1)}) fusion(bf16[384,128]{1,0:T(8,128)(2,1)S(1)} %select_reduce_fusion, bf16[128,63,128]{2,0,1:T(8,128)(2,1)S(1)} %get-tuple-element.20, bf16[128,63,128]{2,0,1:T(8,128)(2,1)S(1)} %get-tuple-element.19, bf16[128,64,128]{2,0,1:T(8,128)(2,1)S(1)} %bitcast.881), kind=kOutput, calls=%fused_computation.55 | convolution fusion | flops 838860672 | bytes 10519040 | tf_op jit(solution)/shard_map/cbr,rt->cbt/dot_general | solution.py:50
  43.6 1.5 fusion.122
  45.1 2.7 %multiply_reduce_fusion = (f32[128]{0:T(128)S(1)}, f32[128,64,128]{0,2,1:T(8,128)S(1)}) fusion(bf16[384,128]{1,0:T(8,128)(2,1)S(1)} %select_reduce_fusion, bf16[128,63,128]{2,0,1:T(8,128)(2,1)S(1)} %get-tuple-element.22, bf16[128,63,128]{2,0,1:T(8,128)(2,1)S(1)} %get-tuple-element.21, bf16[128,64,128]{2,0,1:T(8,128)(2,1)S(1)} %bitcast.879), kind=kOutput, calls=%fused_computation.53 | convolution fusion | flops 838860672 | bytes 10519040 | tf_op jit(solution)/shard_map/cbr,rt->cbt/dot_general | solution.py:50
  50.2 1.5 fusion.120
  51.7 2.7 %multiply_reduce_fusion.2 = (f32[128]{0:T(128)S(1)}, f32[128,64,128]{0,2,1:T(8,128)S(1)}) fusion(bf16[384,128]{1,0:T(8,128)(2,1)S(1)} %select_reduce_fusion, bf16[128,63,128]{2,0,1:T(8,128)(2,1)S(1)} %get-tuple-element.18, bf16[128,63,128]{2,0,1:T(8,128)(2,1)S(1)} %get-tuple-element.17, bf16[128,64,128]{2,0,1:T(8,128)(2,1)S(1)} %bitcast.877), kind=kOutput, calls=%fused_computation.57 | convolution fusion | flops 838860672 | bytes 10519040 | tf_op jit(solution)/shard_map/cbr,rt->cbt/dot_general | solution.py:50
  54.4 2.0 copy-done.2
  56.3 1.0 multiply_convert_fusion.5
  59.0 5.6 %copy.33 = f32[128,8192]{1,0:T(8,128)} copy(f32[128,8192]{0,1:T(8,128)} %bitcast.884) | data formatting | bytes 8388608 | tf_op jit(solution)/shard_map/reshape | solution.py:51
  64.6 5.6 %copy.37 = f32[128,8192]{1,0:T(8,128)} copy(f32[128,8192]{0,1:T(8,128)} %bitcast.883) | data formatting | bytes 8388608 | tf_op jit(solution)/shard_map/reshape | solution.py:51
  70.1 5.6 %copy.35 = f32[128,8192]{1,0:T(8,128)} copy(f32[128,8192]{0,1:T(8,128)} %bitcast.882) | data formatting | bytes 8388608 | tf_op jit(solution)/shard_map/reshape | solution.py:51
  75.8 42.3 %all-reduce.13.cloned.1.call-done = bf16[3,4,8192]{2,1,0:T(4,128)(2,1)} async-done(((bf16[3,4,8192]{2,1,0:T(4,128)(2,1)}), bf16[3,4,8192]{2,1,0:T(4,128)(2,1)}) %all-reduce.13.cloned.1.call-update) | async-done | bytes 196624 | tf_op jit(solution)/shard_map/psum | solution.py:101
  118.1 1.0 slice_bitcast_fusion.11
  167.6 3.2 %copy-done.9 = bf16[4,129,8192]{2,0,1:T(4,128)(2,1)} copy-done((bf16[4,129,8192]{2,0,1:T(4,128)(2,1)}, bf16[4,129,8192]{2,0,1:T(4,128)(2,1)S(1)}, u32[]{:S(2)}) %copy-start.9) | copy-done | bytes 8454168
  170.8 14.1 %fusion.86 = f32[1,4,129,128]{3,2,1,0:T(8,128)} fusion(f32[128,8192]{1,0:T(8,128)S(1)} %copy-done.5, f32[128]{0:T(128)S(1)} %add_rsqrt_fusion.1, bf16[4,129,8192]{2,0,1:T(4,128)(2,1)} %copy-done.9), kind=kOutput, calls=%fused_computation.94 | convolution fusion | flops 1084227584 | bytes 12913152 | tf_op jit(solution)/shard_map/cu,kju->kjc/dot_general | solution.py:65
  184.9 10.4 %fusion.81 = f32[1,4,129,128]{3,2,1,0:T(8,128)} fusion(f32[128,8192]{1,0:T(8,128)S(1)} %copy-done.4, f32[128]{0:T(128)S(1)} %add_rsqrt_fusion.2, bf16[4,129,8192]{2,0,1:T(4,128)(2,1)S(1)} %get-tuple-element.35), kind=kOutput, calls=%fused_computation.93 | convolution fusion | flops 1084227584 | bytes 12913152 | tf_op jit(solution)/shard_map/cu,kju->kjc/dot_general | solution.py:65
  195.3 10.1 %fusion.91 = f32[1,4,129,128]{3,2,1,0:T(8,128)} fusion(f32[128,8192]{1,0:T(8,128)S(1)} %copy-done.3, f32[128]{0:T(128)S(1)} %add_rsqrt_fusion, bf16[4,129,8192]{2,0,1:T(4,128)(2,1)S(1)} %constant_dynamic-update-slice_fusion.258), kind=kOutput, calls=%fused_computation.95 | convolution fusion | flops 1084227584 | bytes 12913152 | tf_op jit(solution)/shard_map/cu,kju->kjc/dot_general | solution.py:65
  205.5 45.2 %all-reduce.15.cloned.1.call-done = (f32[1,4,129,128]{3,2,1,0:T(8,128)}, f32[1,4,129,128]{3,2,1,0:T(8,128)}, f32[1,4,129,128]{3,2,1,0:T(8,128)}) async-done(((f32[1,4,129,128]{3,2,1,0:T(8,128)}, f32[1,4,129,128]{3,2,1,0:T(8,128)}, f32[1,4,129,128]{3,2,1,0:T(8,128)}), (f32[1,4,129,128]{3,2,1,0:T(8,128)}, f32[1,4,129,128]{3,2,1,0:T(8,128)}, f32[1,4,129,128]{3,2,1,0:T(8,128)})) %all-reduce.15.cloned.1.call-update) | async-done | bytes 792592 | tf_op jit(solution)/shard_map/psum | solution.py:104
  250.7 1.2 maximum_multiply_fusion
  251.9 1.1 copy.39
  (436 shorter events, 53.6 us)
Async XLA Ops:
  6.5 21.7 %copy-start.10 = (f32[33]{0:T(128)S(1)}, f32[33]{0:T(128)}, u32[]{:S(2)}) copy-start(f32[33]{0:T(128)} %param.5) | copy-start | bytes 400
  6.5 21.7 %copy-start.11 = (f32[65]{0:T(128)S(1)}, f32[65]{0:T(128)}, u32[]{:S(2)}) copy-start(f32[65]{0:T(128)} %param.6) | copy-start | bytes 784
  6.5 21.8 %copy-start.8 = (s32[3,4]{1,0:T(4,128)S(1)}, s32[3,4]{1,0:T(4,128)}, u32[]{:S(2)}) copy-start(s32[3,4]{1,0:T(4,128)} %param.7) | copy-start | bytes 148
  6.5 111.5 %all-reduce.13.cloned.1.call-start = ((), (), s32[]{:S(2)}) async-start(), calls=%async_computation | async-start | bytes 393216 | tf_op jit(solution)/shard_map/psum | solution.py:101
  8.8 21.4 %collective-permute-start = (bf16[16,8192]{1,0:T(8,128)(2,1)}, bf16[16,8192]{1,0:T(8,128)(2,1)}, u32[]{:S(2)}, u32[]{:S(2)}) collective-permute-start(bf16[16,8192]{1,0:T(8,128)(2,1)} %get-tuple-element.8), channel_id=1, source_target_pairs={{0,4},{4,8},{8,12},{12,16},{16,20},{20,24},{24,28},{1,5},{5,9},{9,... | collective-permute-start | bytes 786440 | tf_op jit(solution)/shard_map/ppermute | solution.py:19
  11.9 22.9 %collective-permute-start.4 = (bf16[16,8192]{1,0:T(8,128)(2,1)S(1)}, bf16[16,8192]{1,0:T(8,128)(2,1)}, u32[]{:S(2)}, u32[]{:S(2)}) collective-permute-start(bf16[16,8192]{1,0:T(8,128)(2,1)S(1)} %get-tuple-element.9), channel_id=1, source_target_pairs={{0,4},{4,8},{8,12},{12,16},{16,20},{20,24},{24,28},{1,5},{5,9},{9,... | collective-permute-start | bytes 786440 | tf_op jit(solution)/shard_map/ppermute | solution.py:19
  16.4 20.7 %collective-permute-start.3 = (bf16[16,8192]{1,0:T(8,128)(2,1)S(1)}, bf16[16,8192]{1,0:T(8,128)(2,1)}, u32[]{:S(2)}, u32[]{:S(2)}) collective-permute-start(bf16[16,8192]{1,0:T(8,128)(2,1)S(1)} %get-tuple-element.10), channel_id=1, source_target_pairs={{4,0},{8,4},{12,8},{16,12},{20,16},{24,20},{28,24},{5,1},{9,5},{13... | collective-permute-start | bytes 786440 | tf_op jit(solution)/shard_map/ppermute | solution.py:21
  17.7 19.4 %collective-permute-start.2 = (bf16[16,8192]{1,0:T(8,128)(2,1)S(1)}, bf16[16,8192]{1,0:T(8,128)(2,1)}, u32[]{:S(2)}, u32[]{:S(2)}) collective-permute-start(bf16[16,8192]{1,0:T(8,128)(2,1)S(1)} %get-tuple-element.11), channel_id=1, source_target_pairs={{0,4},{4,8},{8,12},{12,16},{16,20},{20,24},{24,28},{1,5},{5,9},{9,... | collective-permute-start | bytes 786440 | tf_op jit(solution)/shard_map/ppermute | solution.py:19
  21.5 10.3 %collective-permute-start.1 = (bf16[16,8192]{1,0:T(8,128)(2,1)}, bf16[16,8192]{1,0:T(8,128)(2,1)}, u32[]{:S(2)}, u32[]{:S(2)}) collective-permute-start(bf16[16,8192]{1,0:T(8,128)(2,1)} %get-tuple-element.12), channel_id=1, source_target_pairs={{4,0},{8,4},{12,8},{16,12},{20,16},{24,20},{28,24},{5,1},{9,5},{13... | collective-permute-start | bytes 786440 | tf_op jit(solution)/shard_map/ppermute | solution.py:21
  28.4 6.5 %copy-start.6 = (bf16[128,8192]{1,0:T(8,128)(2,1)S(1)}, bf16[128,8192]{1,0:T(8,128)(2,1)}, u32[]{:S(2)}) copy-start(bf16[128,8192]{1,0:T(8,128)(2,1)} %get-tuple-element.16) | copy-start | bytes 6291460
  30.2 4.6 %collective-permute-start.5 = (bf16[16,8192]{1,0:T(8,128)(2,1)S(1)}, bf16[16,8192]{1,0:T(8,128)(2,1)S(1)}, u32[]{:S(2)}, u32[]{:S(2)}) collective-permute-start(bf16[16,8192]{1,0:T(8,128)(2,1)S(1)} %get-tuple-element.13), channel_id=1, source_target_pairs={{4,0},{8,4},{12,8},{16,12},{20,16},{24,20},{28,24},{5,1},{9,5},{13... | collective-permute-start | bytes 786440 | tf_op jit(solution)/shard_map/ppermute | solution.py:21
  43.6 4.2 %copy-start = (f32[128,64,128]{0,2,1:T(8,128)}, f32[128,64,128]{0,2,1:T(8,128)S(1)}, u32[]{:S(2)}) copy-start(f32[128,64,128]{0,2,1:T(8,128)S(1)} %get-tuple-element.32) | copy-start | bytes 12582916
  47.8 2.4 copy-start.1
  54.4 2.0 copy-start.2
  58.9 191.8 %all-reduce.15.cloned.1.call-start = ((), (), s32[]{:S(2)}) async-start(), calls=%async_computation.1 | async-start | bytes 1671168 | tf_op jit(solution)/shard_map/psum | solution.py:104
  127.0 16.3 %copy-start.7 = (bf16[3,4,8192]{2,1,0:T(4,128)(2,1)S(1)}, bf16[3,4,8192]{2,1,0:T(4,128)(2,1)}, u32[]{:S(2)}) copy-start(bf16[3,4,8192]{2,1,0:T(4,128)(2,1)} %all-reduce.13.cloned.1.call-done) | copy-start | bytes 589828
  151.3 19.5 %copy-start.5 = (f32[128,8192]{1,0:T(8,128)S(1)}, f32[128,8192]{1,0:T(8,128)}, u32[]{:S(2)}) copy-start(f32[128,8192]{1,0:T(8,128)} %copy.35) | copy-start | bytes 12582916
  166.5 18.4 %copy-start.4 = (f32[128,8192]{1,0:T(8,128)S(1)}, f32[128,8192]{1,0:T(8,128)}, u32[]{:S(2)}) copy-start(f32[128,8192]{1,0:T(8,128)} %copy.33) | copy-start | bytes 12582916
  167.6 3.3 %copy-start.9 = (bf16[4,129,8192]{2,0,1:T(4,128)(2,1)}, bf16[4,129,8192]{2,0,1:T(4,128)(2,1)S(1)}, u32[]{:S(2)}) copy-start(bf16[4,129,8192]{2,0,1:T(4,128)(2,1)S(1)} %get-tuple-element.36) | copy-start | bytes 25362436
  184.9 10.4 %copy-start.3 = (f32[128,8192]{1,0:T(8,128)S(1)}, f32[128,8192]{1,0:T(8,128)}, u32[]{:S(2)}) copy-start(f32[128,8192]{1,0:T(8,128)} %copy.37) | copy-start | bytes 12582916
Sparse Core Ops, SparseCore 0:
  59.0 59.0 all-reduce.12
  205.6 45.0 all-reduce.14
where the time goes:
time: 263 us; the launch traced here: 260 us
  waiting for transfers between devices  87.6 us (33%)
  local copies, waits for them, and re-layouts  85.4 us (32%)
  matrix products  50.3 us (19%)
  starting transfers between devices  15.5 us (6%)
  between operations  15.1 us (6%)
  other arithmetic  6.14 us (2%)
    unnamed x406, local copies, waits for them, and re-layouts  52.3 us
    psum x1, waiting for transfers between devices, body(): summed = jnp.stack([lax.psum(term, 'win') for term in partial_corr])  45.2 us
    psum x1, waiting for transfers between devices, body(): panels = lax.psum(terms.astype(jnp.bfloat16), 'chan')  42.3 us
    dot_general x3, matrix products, correlate(): jnp.einsum('cu,kju->kjc', whitened, shifted, preferred_element_type=jnp.f...  34.6 us
    reshape x3, local copies, waits for them, and re-layouts, time_filter(): return result.reshape(channels_here, samples)  16.8 us
    ppermute x3, starting transfers between devices, padded_2(): lax.ppermute(tail, axis, [(i, (i + 1) % count) for i in range(ends)])  11.4 us
    dot_general x3, matrix products, time_filter(): jnp.einsum('cbr,rt->cbt', extended, weights, preferred_element_type=jnp.f...  7.94 us
    dot_general x3, matrix products, chan_filter(): jnp.dot(band_matrix(tap_table, channels_here, channels_here + 2 * half),...  5.85 us
  transfers between devices with their start and end apart: 8, of which 2 were waited for; matrix products, arithmetic and copies ran while one was open for 11% of the time, Pallas kernels for 0%

commit v1 on v0

--- a/solution.py
+++ b/solution.py
@@ -1,8 +1,11 @@
+import functools
 import math
 
 import jax
 import jax.numpy as jnp
 from jax import lax
+from jax.experimental import pallas as pl
+from jax.experimental.pallas import tpu as pltpu
 from jax.sharding import PartitionSpec as P
 
 LAG = 64
@@ -56,13 +59,53 @@
     return (time_pass * lax.rsqrt(power + 1e-06)).astype(jnp.bfloat16)
 
 
-def correlate(whitened, panel):
-    samples = whitened.shape[1]
-    padded = jnp.pad(panel, ((0, 0), (LAG, LAG)))
-    shifted = jnp.stack(
-        [padded[:, 2 * LAG - j : 2 * LAG - j + samples] for j in range(2 * LAG + 1)], axis=1
-    )
-    return jnp.einsum("cu,kju->kjc", whitened, shifted, preferred_element_type=jnp.float32)
+def corr_body(nb, rows, w_ref, p_ref, o_ref, s_ref):
+    n = pl.program_id(0)
+    k_count = p_ref.shape[0]
+    lanes = 128
+
+    @pl.when(n == 0)
+    def _():
+        o_ref[...] = jnp.zeros_like(o_ref)
+
+    j_idx = lax.broadcasted_iota(jnp.int32, (rows, lanes), 0)
+    r_idx = lax.broadcasted_iota(jnp.int32, (rows, lanes), 1)
+    upper = r_idx >= j_idx
+    for k in range(k_count):
+        rolled = []
+        for b in range(nb + 1):
+            start = pl.multiple_of((n * nb + b) * lanes, lanes)
+            chunk = p_ref[pl.ds(k, 1), pl.ds(start, lanes)]
+            wide = jnp.broadcast_to(chunk, (rows, lanes))
+            rolled.append(pltpu.roll(wide, 0, 1, stride=1, stride_axis=0))
+        for b in range(nb):
+            piece = jnp.where(upper, rolled[b + 1], rolled[b])
+            s_ref[pl.ds(k * rows, rows), pl.ds(b * lanes, lanes)] = piece.astype(s_ref.dtype)
+    o_ref[...] += lax.dot_general(
+        s_ref[...], w_ref[...], (((1,), (1,)), ((), ())),
+        preferred_element_type=jnp.float32)
+
+
+def correlate_kernel(whitened, panel, nb=8):
+    chans, samples = whitened.shape
+    k_count = panel.shape[0]
+    lanes = 128
+    rows = 136
+    padded = jnp.pad(panel.astype(jnp.float32), ((0, 0), (LAG, LAG)))
+    grid = samples // (nb * lanes)
+    out = pl.pallas_call(
+        functools.partial(corr_body, nb, rows),
+        grid=(grid,),
+        in_specs=[
+            pl.BlockSpec((chans, nb * lanes), lambda n: (0, n)),
+            pl.BlockSpec((k_count, samples + 2 * LAG), lambda n: (0, 0)),
+        ],
+        out_specs=pl.BlockSpec((k_count * rows, chans), lambda n: (0, 0)),
+        out_shape=jax.ShapeDtypeStruct((k_count * rows, chans), jnp.float32),
+        scratch_shapes=[pltpu.VMEM((k_count * rows, nb * lanes), jnp.bfloat16)],
+        compiler_params=pltpu.CompilerParams(dimension_semantics=("arbitrary",)),
+    )(whitened, padded)
+    return out.reshape(k_count, rows, chans)[:, : 2 * LAG + 1, :]
 
 
 def chan_filter(piece, tap_table):
@@ -77,6 +120,17 @@
     return total.astype(jnp.bfloat16)
 
 
+def xor_sum(x, axis):
+    count = lax.axis_size(axis)
+    if count & (count - 1):
+        return lax.psum(x, axis)
+    step = 1
+    while step < count:
+        x = x + lax.ppermute(x, axis, [(i, i ^ step) for i in range(count)])
+        step *= 2
+    return x
+
+
 def body(record, chan_taps, time_taps, sources):
     count_steps = record.shape[0]
     channels_here = record.shape[1]
@@ -89,20 +143,14 @@
     ).astype(jnp.bfloat16)
     normalizer = 1.0 / math.sqrt(samples * lax.axis_size("win"))
 
-    def prepare(section):
-        return whiten(time_filter(chan_filter(record[section], chan_table), time_table))
-
-    def local_panel(whitened, section):
-        return jnp.dot(selector[section], whitened, preferred_element_type=jnp.float32)
-
-    pairs = []
-    prepared = [prepare(section) for section in range(count_steps)]
-    terms = jnp.stack([local_panel(prepared[section], section) for section in range(count_steps)])
-    panels = lax.psum(terms.astype(jnp.bfloat16), "chan")
-    pairs = [(prepared[section], panels[section]) for section in range(count_steps)]
-    partial_corr = [correlate(pair[0], pair[1]) for pair in pairs]
-    summed = jnp.stack([lax.psum(term, "win") for term in partial_corr])
-    return summed * normalizer
+    results = []
+    for section in range(count_steps):
+        whitened = whiten(time_filter(chan_filter(record[section], chan_table), time_table))
+        term = jnp.dot(selector[section], whitened, preferred_element_type=jnp.float32)
+        panel = xor_sum(term.astype(jnp.bfloat16), "chan")
+        partial_corr = correlate_kernel(whitened, panel)
+        results.append(xor_sum(partial_corr, "win"))
+    return jnp.stack(results) * normalizer
 
 
 def solution(mesh):

time: 263 us -> 163 us (0.62)
  waiting for transfers between devices: 87.6 us -> 30.9 us
  local copies, waits for them, and re-layouts: 85.4 us -> 36.4 us
  matrix products: 50.3 us -> 15.9 us
  Pallas kernels: 0 us -> 23.2 us
  starting transfers between devices: 15.5 us -> 35 us
  between operations: 15.1 us -> 0.4 us
  other arithmetic: 6.14 us -> 20.5 us
    psum x2 -> x0, waiting for transfers between devices: 87.5 us -> none  [the longest x1 45.2 us: body(): summed = jnp.stack([lax.psum(term, 'win') for term in partial_corr])]
    unnamed x406 -> x25, local copies, waits for them, and re-layouts: 52.3 us -> 5.62 us
    dot_general x6 -> x3, matrix products: 36.5 us -> 1.93 us  [body(): jnp.dot(selector[section], whitened, preferred_element_type=jnp.float32)]
    ppermute x0 -> x15, waiting for transfers between devices: none -> 30.9 us  [xor_sum(): x = x + lax.ppermute(x, axis, [(i, i ^ step) for i in range(count)])]
    pallas_call x0 -> x3, Pallas kernels: none -> 23.2 us  [correlate_kernel(): pl.pallas_call(functools.partial(corr_body, nb, rows), grid=(grid,), in_s...]
    ppermute x0 -> x15, starting transfers between devices: none -> 18.4 us  [xor_sum(): x = x + lax.ppermute(x, axis, [(i, i ^ step) for i in range(count)])]
    convert_element_type x3 -> x6, other arithmetic: 2.12 us -> 13.4 us  [whiten(): return (time_pass * lax.rsqrt(power + 1e-06)).astype(jnp.bfloat16)]
    squeeze x2 -> x1, local copies, waits for them, and re-layouts: 6.42 us -> 5.51 us  [body(): record[section]]
  transfers between devices with their start and end apart: 8 -> 21, of which waited for: 2 -> 4; matrix products, arithmetic and copies ran while one was open for 11% -> 41% of each run, Pallas kernels for 0% -> 14%
where the time goes in v1:
time: 163 us; the launch traced here: 162 us
  local copies, waits for them, and re-layouts  36.4 us (22%)
  starting transfers between devices  35 us (21%)
  waiting for transfers between devices  30.9 us (19%)
  Pallas kernels  23.2 us (14%)
  other arithmetic  20.5 us (13%)
  matrix products  15.9 us (10%)
    ppermute x15, waiting for transfers between devices, xor_sum(): x = x + lax.ppermute(x, axis, [(i, i ^ step) for i in range(count)])  30.9 us
    pallas_call x3, Pallas kernels, correlate_kernel(): pl.pallas_call(functools.partial(corr_body, nb, rows), grid=(grid,), in_s...  23.2 us
    ppermute x15, starting transfers between devices, xor_sum(): x = x + lax.ppermute(x, axis, [(i, i ^ step) for i in range(count)])  18.4 us
    reshape x3, local copies, waits for them, and re-layouts, time_filter(): return result.reshape(channels_here, samples)  16.9 us
    convert_element_type x6, other arithmetic, whiten(): return (time_pass * lax.rsqrt(power + 1e-06)).astype(jnp.bfloat16)  13.4 us
    ppermute x3, starting transfers between devices, padded_2(): lax.ppermute(tail, axis, [(i, (i + 1) % count) for i in range(ends)])  12.7 us
    dot_general x3, matrix products, time_filter(): jnp.einsum('cbr,rt->cbt', extended, weights, preferred_element_type=jnp.f...  7.98 us
    dot_general x3, matrix products, chan_filter(): jnp.dot(band_matrix(tap_table, channels_here, channels_here + 2 * half),...  5.94 us
  transfers between devices with their start and end apart: 21, of which 4 were waited for; matrix products, arithmetic and copies ran while one was open for 41% of the time, Pallas kernels for 14%

profile of v1, /device:TPU:0, one launch (start us, length us, event | category | flops | bytes accessed | tf_op | source)
XLA Modules:
  0.0 162.3 jit_solution(4205313927144105256)
XLA Ops:
  0.0 2.2 %slice_bitcast_fusion.8 = (bf16[16,8192]{1,0:T(8,128)(2,1)}, bf16[16,8192]{1,0:T(8,128)(2,1)S(1)}, bf16[16,8192]{1,0:T(8,128)(2,1)S(1)}, bf16[16,8192]{1,0:T(8,1...) fusion(bf16[3,128,8192]{2,1,0:T(8,128)(2,1)} %param.4), kind=kLoop, calls=%fused_computation.87 | loop fusion | bytes 3145728 | tf_op jit(solution)/shard_map/slice | solution.py:19
  2.2 3.1 %collective-permute-start = (bf16[16,8192]{1,0:T(8,128)(2,1)}, bf16[16,8192]{1,0:T(8,128)(2,1)}, u32[]{:S(2)}, u32[]{:S(2)}) collective-permute-start(bf16[16,8192]{1,0:T(8,128)(2,1)} %get-tuple-element.5), channel_id=1, source_target_pairs={{0,4},{4,8},{8,12},{12,16},{16,20},{20,24},{24,28},{1,5},{5,9},{9,... | collective-permute-start | bytes 786440 | tf_op jit(solution)/shard_map/ppermute | solution.py:22
  6.6 5.1 %collective-permute-start.7 = (bf16[16,8192]{1,0:T(8,128)(2,1)S(1)}, bf16[16,8192]{1,0:T(8,128)(2,1)}, u32[]{:S(2)}, u32[]{:S(2)}) collective-permute-start(bf16[16,8192]{1,0:T(8,128)(2,1)S(1)} %get-tuple-element.8), channel_id=1, source_target_pairs={{0,4},{4,8},{8,12},{12,16},{16,20},{20,24},{24,28},{1,5},{5,9},{9,... | collective-permute-start | bytes 786440 | tf_op jit(solution)/shard_map/ppermute | solution.py:22
  13.1 4.4 %collective-permute-start.14 = (bf16[16,8192]{1,0:T(8,128)(2,1)S(1)}, bf16[16,8192]{1,0:T(8,128)(2,1)}, u32[]{:S(2)}, u32[]{:S(2)}) collective-permute-start(bf16[16,8192]{1,0:T(8,128)(2,1)S(1)} %get-tuple-element.6), channel_id=1, source_target_pairs={{0,4},{4,8},{8,12},{12,16},{16,20},{20,24},{24,28},{1,5},{5,9},{9,... | collective-permute-start | bytes 786440 | tf_op jit(solution)/shard_map/ppermute | solution.py:22
  17.5 5.5 %slice_bitcast_fusion.2 = (bf16[128,8192]{1,0:T(8,128)(2,1)}, bf16[128,8192]{1,0:T(8,128)(2,1)}, bf16[128,8192]{1,0:T(8,128)(2,1)S(1)}) fusion(bf16[3,128,8192]{2,1,0:T(8,128)(2,1)} %param.4), kind=kLoop, calls=%fused_computation.74 | loop fusion | bytes 12582912 | tf_op jit(solution)/shard_map/squeeze | solution.py:148
  26.4 2.4 %fusion.54 = bf16[16,64,8,128]{3,2,1,0:T(8,128)(2,1)S(1)} fusion(bf16[16,8192]{1,0:T(8,128)(2,1)} %collective-permute-done.1, bf16[128,8192]{1,0:T(8,128)(2,1)} %get-tuple-element.11, bf16[16,8192]{1,0:T(8,128)(2,1)} %collective-permute-done, bf16[128,160]{0,1:T(8,128)(2,1)S(1)} %select_reduce_fusion.1), kind=kOutput, calls=%fused_computation.75 | convolution fusion | flops 344457216 | bytes 4759552 | tf_op jit(solution)/shard_map/dot_general | solution.py:115
  29.4 1.5 fusion.87
  30.9 2.7 %multiply_reduce_fusion.2 = (f32[128]{0:T(128)S(1)}, f32[128,64,128]{0,2,1:T(8,128)S(1)}) fusion(bf16[384,128]{1,0:T(8,128)(2,1)S(1)} %select_reduce_fusion, bf16[128,63,128]{2,0,1:T(8,128)(2,1)S(1)} %get-tuple-element.15, bf16[128,63,128]{2,0,1:T(8,128)(2,1)S(1)} %get-tuple-element.14, bf16[128,64,128]{2,0,1:T(8,128)(2,1)S(1)} %bitcast.84), kind=kOutput, calls=%fused_computation.48 | convolution fusion | flops 838860672 | bytes 10519040 | tf_op jit(solution)/shard_map/cbr,rt->cbt/dot_general | solution.py:53
  35.6 1.7 %collective-permute-start.2 = (bf16[4,8192]{1,0:T(4,128)(2,1)S(1)}, bf16[4,8192]{1,0:T(4,128)(2,1)S(1)}, u32[]{:S(2)}, u32[]{:S(2)}) collective-permute-start(bf16[4,8192]{1,0:T(4,128)(2,1)S(1)} %convolution_convert_fusion.5), channel_id=1, source_target_pairs={{0,4},{4,0},{8,12},{12,8},{16,20},{20,16},{24,28},{28,24},{1,5},{5... | collective-permute-start | bytes 196616 | tf_op jit(solution)/shard_map/ppermute | solution.py:129
  37.2 5.6 %copy.42 = f32[128,8192]{1,0:T(8,128)} copy(f32[128,8192]{0,1:T(8,128)} %bitcast.89) | data formatting | bytes 8388608 | tf_op jit(solution)/shard_map/reshape | solution.py:54
  42.9 4.0 %multiply_convert_fusion.5.w_ref = bf16[128,8192]{1,0:T(8,128)(2,1)} fusion(f32[128,8192]{1,0:T(8,128)} %copy.42, f32[128]{0:T(128)S(1)} %add_rsqrt_fusion.2), kind=kLoop, calls=%fused_computation.47 | loop fusion | flops 2097152 | bytes 6291968 | tf_op jit(solution)/shard_map/convert_element_type | solution.py:59
  46.9 1.8 %fusion.57 = bf16[16,64,8,128]{3,2,1,0:T(8,128)(2,1)S(1)} fusion(bf16[16,8192]{1,0:T(8,128)(2,1)} %collective-permute-done.8, bf16[128,8192]{1,0:T(8,128)(2,1)S(1)} %copy-done.5, bf16[16,8192]{1,0:T(8,128)(2,1)} %collective-permute-done.7, bf16[128,160]{0,1:T(8,128)(2,1)S(1)} %select_reduce_fusion.1), kind=kOutput, calls=%fused_computation.76 | convolution fusion | flops 344457216 | bytes 4759552 | tf_op jit(solution)/shard_map/dot_general | solution.py:115
  49.3 1.5 fusion.88
  50.7 2.7 %multiply_reduce_fusion.1 = (f32[128]{0:T(128)S(1)}, f32[128,64,128]{0,2,1:T(8,128)S(1)}) fusion(bf16[384,128]{1,0:T(8,128)(2,1)S(1)} %select_reduce_fusion, bf16[128,63,128]{2,0,1:T(8,128)(2,1)S(1)} %get-tuple-element.17, bf16[128,63,128]{2,0,1:T(8,128)(2,1)S(1)} %get-tuple-element.16, bf16[128,64,128]{2,0,1:T(8,128)(2,1)S(1)} %bitcast.86), kind=kOutput, calls=%fused_computation.45 | convolution fusion | flops 838860672 | bytes 10519040 | tf_op jit(solution)/shard_map/cbr,rt->cbt/dot_general | solution.py:53
  55.4 1.8 %fusion.60 = bf16[16,64,8,128]{3,2,1,0:T(8,128)(2,1)S(1)} fusion(bf16[16,8192]{1,0:T(8,128)(2,1)} %collective-permute-done.15, bf16[128,8192]{1,0:T(8,128)(2,1)S(1)} %get-tuple-element.13, bf16[16,8192]{1,0:T(8,128)(2,1)} %collective-permute-done.14, bf16[128,160]{0,1:T(8,128)(2,1)S(1)} %copy-done.7), kind=kOutput, calls=%fused_computation.77 | convolution fusion | flops 344457216 | bytes 4759552 | tf_op jit(solution)/shard_map/dot_general | solution.py:115
  59.3 2.7 %multiply_reduce_fusion = (f32[128]{0:T(128)S(1)}, f32[128,64,128]{0,2,1:T(8,128)S(1)}) fusion(bf16[384,128]{1,0:T(8,128)(2,1)S(1)} %select_reduce_fusion, bf16[128,63,128]{2,0,1:T(8,128)(2,1)S(1)} %get-tuple-element.19, bf16[128,63,128]{2,0,1:T(8,128)(2,1)S(1)} %get-tuple-element.18, bf16[128,64,128]{2,0,1:T(8,128)(2,1)S(1)} %bitcast.82), kind=kOutput, calls=%fused_computation.42 | convolution fusion | flops 838860672 | bytes 10519040 | tf_op jit(solution)/shard_map/cbr,rt->cbt/dot_general | solution.py:53
  63.9 5.6 %copy.44 = f32[128,8192]{1,0:T(8,128)} copy(f32[128,8192]{0,1:T(8,128)} %bitcast.87) | data formatting | bytes 8388608 | tf_op jit(solution)/shard_map/reshape | solution.py:54
  70.1 3.3 %collective-permute-start.3 = (bf16[4,8192]{1,0:T(4,128)(2,1)S(1)}, bf16[4,8192]{1,0:T(4,128)(2,1)S(1)}, u32[]{:S(2)}, u32[]{:S(2)}) collective-permute-start(bf16[4,8192]{1,0:T(4,128)(2,1)S(1)} %add.104), channel_id=1, source_target_pairs={{0,8},{4,12},{8,0},{12,4},{16,24},{20,28},{24,16},{28,20},{1,9},{5... | collective-permute-start | bytes 196616 | tf_op jit(solution)/shard_map/ppermute | solution.py:129
  73.4 3.9 %multiply_convert_fusion.3.w_ref = bf16[128,8192]{1,0:T(8,128)(2,1)} fusion(f32[128,8192]{1,0:T(8,128)} %copy.44, f32[128]{0:T(128)S(1)} %add_rsqrt_fusion.1), kind=kLoop, calls=%fused_computation.44 | loop fusion | flops 2097152 | bytes 6291968 | tf_op jit(solution)/shard_map/convert_element_type | solution.py:59
  77.3 5.6 %copy.46 = f32[128,8192]{1,0:T(8,128)} copy(f32[128,8192]{0,1:T(8,128)} %bitcast.88) | data formatting | bytes 8388608 | tf_op jit(solution)/shard_map/reshape | solution.py:54
  83.1 2.1 %collective-permute-start.17 = (bf16[4,8192]{1,0:T(4,128)(2,1)S(1)}, bf16[4,8192]{1,0:T(4,128)(2,1)S(1)}, u32[]{:S(2)}, u32[]{:S(2)}) collective-permute-start(bf16[4,8192]{1,0:T(4,128)(2,1)S(1)} %add.116), channel_id=1, source_target_pairs={{0,8},{4,12},{8,0},{12,4},{16,24},{20,28},{24,16},{28,20},{1,9},{5... | collective-permute-start | bytes 196616 | tf_op jit(solution)/shard_map/ppermute | solution.py:129
  86.4 3.9 %multiply_convert_fusion.1.w_ref = bf16[128,8192]{1,0:T(8,128)(2,1)} fusion(f32[128,8192]{1,0:T(8,128)} %copy.46, f32[128]{0:T(128)S(1)} %add_rsqrt_fusion), kind=kLoop, calls=%fused_computation.41 | loop fusion | flops 2097152 | bytes 6291968 | tf_op jit(solution)/shard_map/convert_element_type | solution.py:59
  93.3 7.7 %shard_map.46 = f32[544,128]{1,0:T(8,128)} custom-call(bf16[128,8192]{1,0:T(8,128)(2,1)} %multiply_convert_fusion.5.w_ref, f32[4,8320]{1,0:T(4,128)} %pad_convert_fusion.2.p_ref), custom_call_target="tpu_custom_call" | custom-call | tf_op jit(solution)/shard_map/pallas_call | solution.py:96
  102.2 1.6 %collective-permute-start.5 = (f32[4,129,128]{2,0,1:T(4,128)S(1)}, f32[4,129,128]{2,0,1:T(4,128)S(1)}, u32[]{:S(2)}, u32[]{:S(2)}) collective-permute-start(f32[4,129,128]{2,0,1:T(4,128)S(1)} %copy.47), channel_id=1, source_target_pairs={{0,1},{1,0},{2,3},{3,2},{4,5},{5,4},{6,7},{7,6},{8,9},{9,8},{10,11... | collective-permute-start | bytes 792584 | tf_op jit(solution)/shard_map/ppermute | solution.py:129
  104.6 7.7 %shard_map.47 = f32[544,128]{1,0:T(8,128)} custom-call(bf16[128,8192]{1,0:T(8,128)(2,1)} %multiply_convert_fusion.3.w_ref, f32[4,8320]{1,0:T(4,128)} %pad_convert_fusion.1.p_ref), custom_call_target="tpu_custom_call" | custom-call | tf_op jit(solution)/shard_map/pallas_call | solution.py:96
  114.8 7.7 %shard_map.48 = f32[544,128]{1,0:T(8,128)} custom-call(bf16[128,8192]{1,0:T(8,128)(2,1)} %multiply_convert_fusion.1.w_ref, f32[4,8320]{1,0:T(4,128)} %pad_convert_fusion.p_ref), custom_call_target="tpu_custom_call" | custom-call | tf_op jit(solution)/shard_map/pallas_call | solution.py:96
  123.5 1.6 %collective-permute-start.19 = (f32[4,129,128]{2,0,1:T(4,128)S(1)}, f32[4,129,128]{2,0,1:T(4,128)S(1)}, u32[]{:S(2)}, u32[]{:S(2)}) collective-permute-start(f32[4,129,128]{2,0,1:T(4,128)S(1)} %copy.49), channel_id=1, source_target_pairs={{0,1},{1,0},{2,3},{3,2},{4,5},{5,4},{6,7},{7,6},{8,9},{9,8},{10,11... | collective-permute-start | bytes 792584 | tf_op jit(solution)/shard_map/ppermute | solution.py:129
  125.3 2.7 %collective-permute-start.6 = (f32[4,129,128]{2,0,1:T(4,128)S(1)}, f32[4,129,128]{2,0,1:T(4,128)S(1)}, u32[]{:S(2)}, u32[]{:S(2)}) collective-permute-start(f32[4,129,128]{2,0,1:T(4,128)S(1)} %copy_add_fusion), channel_id=1, source_target_pairs={{0,2},{1,3},{2,0},{3,1},{4,6},{5,7},{6,4},{7,5},{8,10},{9,11},{10,... | collective-permute-start | bytes 792584 | tf_op jit(solution)/shard_map/ppermute | solution.py:129
  128.4 7.4 %collective-permute-done.19 = f32[4,129,128]{2,0,1:T(4,128)S(1)} collective-permute-done((f32[4,129,128]{2,0,1:T(4,128)S(1)}, f32[4,129,128]{2,0,1:T(4,128)S(1)}, u32[]{:S(2)}, u32[]{:S(2)}) %collective-permute-start.19) | collective-permute-done | bytes 264224 | tf_op jit(solution)/shard_map/ppermute | solution.py:129
  137.4 15.0 %collective-permute-done.6 = f32[4,129,128]{2,0,1:T(4,128)S(1)} collective-permute-done((f32[4,129,128]{2,0,1:T(4,128)S(1)}, f32[4,129,128]{2,0,1:T(4,128)S(1)}, u32[]{:S(2)}, u32[]{:S(2)}) %collective-permute-start.6) | collective-permute-done | bytes 264224 | tf_op jit(solution)/shard_map/ppermute | solution.py:129
  152.5 5.6 %collective-permute-done.13 = f32[4,129,128]{2,0,1:T(4,128)S(1)} collective-permute-done((f32[4,129,128]{2,0,1:T(4,128)S(1)}, f32[4,129,128]{2,0,1:T(4,128)S(1)}, u32[]{:S(2)}, u32[]{:S(2)}) %collective-permute-start.13) | collective-permute-done | bytes 264224 | tf_op jit(solution)/shard_map/ppermute | solution.py:129
  158.2 2.9 %collective-permute-done.20 = f32[4,129,128]{2,0,1:T(4,128)S(1)} collective-permute-done((f32[4,129,128]{2,0,1:T(4,128)S(1)}, f32[4,129,128]{2,0,1:T(4,128)S(1)}, u32[]{:S(2)}, u32[]{:S(2)}) %collective-permute-start.20) | collective-permute-done | bytes 264224 | tf_op jit(solution)/shard_map/ppermute | solution.py:129
  (95 shorter events, 28.9 us)
Async XLA Ops:
  2.2 22.8 %collective-permute-start = (bf16[16,8192]{1,0:T(8,128)(2,1)}, bf16[16,8192]{1,0:T(8,128)(2,1)}, u32[]{:S(2)}, u32[]{:S(2)}) collective-permute-start(bf16[16,8192]{1,0:T(8,128)(2,1)} %get-tuple-element.5), channel_id=1, source_target_pairs={{0,4},{4,8},{8,12},{12,16},{16,20},{20,24},{24,28},{1,5},{5,9},{9,... | collective-permute-start | bytes 786440 | tf_op jit(solution)/shard_map/ppermute | solution.py:22
  5.3 21.0 %collective-permute-start.1 = (bf16[16,8192]{1,0:T(8,128)(2,1)}, bf16[16,8192]{1,0:T(8,128)(2,1)}, u32[]{:S(2)}, u32[]{:S(2)}) collective-permute-start(bf16[16,8192]{1,0:T(8,128)(2,1)} %get-tuple-element.9), channel_id=1, source_target_pairs={{4,0},{8,4},{12,8},{16,12},{20,16},{24,20},{28,24},{5,1},{9,5},{13... | collective-permute-start | bytes 786440 | tf_op jit(solution)/shard_map/ppermute | solution.py:24
  6.6 40.2 %collective-permute-start.7 = (bf16[16,8192]{1,0:T(8,128)(2,1)S(1)}, bf16[16,8192]{1,0:T(8,128)(2,1)}, u32[]{:S(2)}, u32[]{:S(2)}) collective-permute-start(bf16[16,8192]{1,0:T(8,128)(2,1)S(1)} %get-tuple-element.8), channel_id=1, source_target_pairs={{0,4},{4,8},{8,12},{12,16},{16,20},{20,24},{24,28},{1,5},{5,9},{9,... | collective-permute-start | bytes 786440 | tf_op jit(solution)/shard_map/ppermute | solution.py:22
  11.8 35.1 %collective-permute-start.8 = (bf16[16,8192]{1,0:T(8,128)(2,1)S(1)}, bf16[16,8192]{1,0:T(8,128)(2,1)}, u32[]{:S(2)}, u32[]{:S(2)}) collective-permute-start(bf16[16,8192]{1,0:T(8,128)(2,1)S(1)} %get-tuple-element.7), channel_id=1, source_target_pairs={{4,0},{8,4},{12,8},{16,12},{20,16},{24,20},{28,24},{5,1},{9,5},{13... | collective-permute-start | bytes 786440 | tf_op jit(solution)/shard_map/ppermute | solution.py:24
  13.0 10.0 %copy-start.9 = (f32[33]{0:T(128)S(1)}, f32[33]{0:T(128)}, u32[]{:S(2)}) copy-start(f32[33]{0:T(128)} %param.5) | copy-start | bytes 400
  13.1 10.1 %copy-start.10 = (f32[65]{0:T(128)S(1)}, f32[65]{0:T(128)}, u32[]{:S(2)}) copy-start(f32[65]{0:T(128)} %param.6) | copy-start | bytes 784
  13.1 11.6 %copy-start.8 = (s32[3,4]{1,0:T(4,128)S(1)}, s32[3,4]{1,0:T(4,128)}, u32[]{:S(2)}) copy-start(s32[3,4]{1,0:T(4,128)} %param.7) | copy-start | bytes 148
  13.1 42.4 %collective-permute-start.14 = (bf16[16,8192]{1,0:T(8,128)(2,1)S(1)}, bf16[16,8192]{1,0:T(8,128)(2,1)}, u32[]{:S(2)}, u32[]{:S(2)}) collective-permute-start(bf16[16,8192]{1,0:T(8,128)(2,1)S(1)} %get-tuple-element.6), channel_id=1, source_target_pairs={{0,4},{4,8},{8,12},{12,16},{16,20},{20,24},{24,28},{1,5},{5,9},{9,... | collective-permute-start | bytes 786440 | tf_op jit(solution)/shard_map/ppermute | solution.py:22
  25.0 21.9 %copy-start.6 = (bf16[128,160]{0,1:T(8,128)(2,1)}, bf16[128,160]{0,1:T(8,128)(2,1)S(1)}, u32[]{:S(2)}) copy-start(bf16[128,160]{0,1:T(8,128)(2,1)S(1)} %select_reduce_fusion.1) | copy-start | bytes 122884
  25.1 30.4 %collective-permute-start.15 = (bf16[16,8192]{1,0:T(8,128)(2,1)S(1)}, bf16[16,8192]{1,0:T(8,128)(2,1)}, u32[]{:S(2)}, u32[]{:S(2)}) collective-permute-start(bf16[16,8192]{1,0:T(8,128)(2,1)S(1)} %get-tuple-element.10), channel_id=1, source_target_pairs={{4,0},{8,4},{12,8},{16,12},{20,16},{24,20},{28,24},{5,1},{9,5},{13... | collective-permute-start | bytes 786440 | tf_op jit(solution)/shard_map/ppermute | solution.py:24
  33.5 2.0 %copy-start.2 = (f32[128,64,128]{0,2,1:T(8,128)}, f32[128,64,128]{0,2,1:T(8,128)S(1)}, u32[]{:S(2)}) copy-start(f32[128,64,128]{0,2,1:T(8,128)S(1)} %get-tuple-element.25) | copy-start | bytes 12582916
  35.6 34.5 %collective-permute-start.2 = (bf16[4,8192]{1,0:T(4,128)(2,1)S(1)}, bf16[4,8192]{1,0:T(4,128)(2,1)S(1)}, u32[]{:S(2)}, u32[]{:S(2)}) collective-permute-start(bf16[4,8192]{1,0:T(4,128)(2,1)S(1)} %convolution_convert_fusion.5), channel_id=1, source_target_pairs={{0,4},{4,0},{8,12},{12,8},{16,20},{20,16},{24,28},{28,24},{1,5},{5... | collective-permute-start | bytes 196616 | tf_op jit(solution)/shard_map/ppermute | solution.py:129
  42.9 4.0 %copy-start.5 = (bf16[128,8192]{1,0:T(8,128)(2,1)S(1)}, bf16[128,8192]{1,0:T(8,128)(2,1)}, u32[]{:S(2)}) copy-start(bf16[128,8192]{1,0:T(8,128)(2,1)} %get-tuple-element.12) | copy-start | bytes 6291460
  53.4 2.0 %copy-start = (f32[128,64,128]{0,2,1:T(8,128)}, f32[128,64,128]{0,2,1:T(8,128)S(1)}, u32[]{:S(2)}) copy-start(f32[128,64,128]{0,2,1:T(8,128)S(1)} %get-tuple-element.23) | copy-start | bytes 12582916
  53.4 2.0 %copy-start.7 = (bf16[128,160]{0,1:T(8,128)(2,1)S(1)}, bf16[128,160]{0,1:T(8,128)(2,1)}, u32[]{:S(2)}) copy-start(bf16[128,160]{0,1:T(8,128)(2,1)} %copy-done.6) | copy-start | bytes 122884
  55.4 27.5 %collective-permute-start.9 = (bf16[4,8192]{1,0:T(4,128)(2,1)S(1)}, bf16[4,8192]{1,0:T(4,128)(2,1)S(1)}, u32[]{:S(2)}, u32[]{:S(2)}) collective-permute-start(bf16[4,8192]{1,0:T(4,128)(2,1)S(1)} %convolution_convert_fusion.4), channel_id=1, source_target_pairs={{0,4},{4,0},{8,12},{12,8},{16,20},{20,16},{24,28},{28,24},{1,5},{5... | collective-permute-start | bytes 196616 | tf_op jit(solution)/shard_map/ppermute | solution.py:129
  62.0 1.9 %copy-start.1 = (f32[128,64,128]{0,2,1:T(8,128)}, f32[128,64,128]{0,2,1:T(8,128)S(1)}, u32[]{:S(2)}) copy-start(f32[128,64,128]{0,2,1:T(8,128)S(1)} %get-tuple-element.21) | copy-start | bytes 12582916
  69.5 13.5 %collective-permute-start.16 = (bf16[4,8192]{1,0:T(4,128)(2,1)S(1)}, bf16[4,8192]{1,0:T(4,128)(2,1)S(1)}, u32[]{:S(2)}, u32[]{:S(2)}) collective-permute-start(bf16[4,8192]{1,0:T(4,128)(2,1)S(1)} %convolution_convert_fusion.3), channel_id=1, source_target_pairs={{0,4},{4,0},{8,12},{12,8},{16,20},{20,16},{24,28},{28,24},{1,5},{5... | collective-permute-start | bytes 196616 | tf_op jit(solution)/shard_map/ppermute | solution.py:129
  70.1 15.1 %collective-permute-start.3 = (bf16[4,8192]{1,0:T(4,128)(2,1)S(1)}, bf16[4,8192]{1,0:T(4,128)(2,1)S(1)}, u32[]{:S(2)}, u32[]{:S(2)}) collective-permute-start(bf16[4,8192]{1,0:T(4,128)(2,1)S(1)} %add.104), channel_id=1, source_target_pairs={{0,8},{4,12},{8,0},{12,4},{16,24},{20,28},{24,16},{28,20},{1,9},{5... | collective-permute-start | bytes 196616 | tf_op jit(solution)/shard_map/ppermute | solution.py:129
  83.0 7.3 %collective-permute-start.10 = (bf16[4,8192]{1,0:T(4,128)(2,1)S(1)}, bf16[4,8192]{1,0:T(4,128)(2,1)S(1)}, u32[]{:S(2)}, u32[]{:S(2)}) collective-permute-start(bf16[4,8192]{1,0:T(4,128)(2,1)S(1)} %add.110), channel_id=1, source_target_pairs={{0,8},{4,12},{8,0},{12,4},{16,24},{20,28},{24,16},{28,20},{1,9},{5... | collective-permute-start | bytes 196616 | tf_op jit(solution)/shard_map/ppermute | solution.py:129
  83.1 8.2 %collective-permute-start.17 = (bf16[4,8192]{1,0:T(4,128)(2,1)S(1)}, bf16[4,8192]{1,0:T(4,128)(2,1)S(1)}, u32[]{:S(2)}, u32[]{:S(2)}) collective-permute-start(bf16[4,8192]{1,0:T(4,128)(2,1)S(1)} %add.116), channel_id=1, source_target_pairs={{0,8},{4,12},{8,0},{12,4},{16,24},{20,28},{24,16},{28,20},{1,9},{5... | collective-permute-start | bytes 196616 | tf_op jit(solution)/shard_map/ppermute | solution.py:129
  85.2 7.3 %collective-permute-start.4 = (bf16[4,8192]{1,0:T(4,128)(2,1)S(1)}, bf16[4,8192]{1,0:T(4,128)(2,1)S(1)}, u32[]{:S(2)}, u32[]{:S(2)}) collective-permute-start(bf16[4,8192]{1,0:T(4,128)(2,1)S(1)} %add.105), channel_id=1, source_target_pairs={{0,16},{4,20},{8,24},{12,28},{16,0},{20,4},{24,8},{28,12},{1,17},{... | collective-permute-start | bytes 196616 | tf_op jit(solution)/shard_map/ppermute | solution.py:129
  90.3 13.5 %collective-permute-start.11 = (bf16[4,8192]{1,0:T(4,128)(2,1)S(1)}, bf16[4,8192]{1,0:T(4,128)(2,1)S(1)}, u32[]{:S(2)}, u32[]{:S(2)}) collective-permute-start(bf16[4,8192]{1,0:T(4,128)(2,1)S(1)} %add.111), channel_id=1, source_target_pairs={{0,16},{4,20},{8,24},{12,28},{16,0},{20,4},{24,8},{28,12},{1,17},{... | collective-permute-start | bytes 196616 | tf_op jit(solution)/shard_map/ppermute | solution.py:129
  91.3 22.6 %collective-permute-start.18 = (bf16[4,8192]{1,0:T(4,128)(2,1)S(1)}, bf16[4,8192]{1,0:T(4,128)(2,1)S(1)}, u32[]{:S(2)}, u32[]{:S(2)}) collective-permute-start(bf16[4,8192]{1,0:T(4,128)(2,1)S(1)} %add.117), channel_id=1, source_target_pairs={{0,16},{4,20},{8,24},{12,28},{16,0},{20,4},{24,8},{28,12},{1,17},{... | collective-permute-start | bytes 196616 | tf_op jit(solution)/shard_map/ppermute | solution.py:129
  101.1 24.1 %copy-start.3 = (f32[544,128]{1,0:T(8,128)S(1)}, f32[544,128]{1,0:T(8,128)}, u32[]{:S(2)}) copy-start(f32[544,128]{1,0:T(8,128)} %shard_map.46) | copy-start | bytes 835588
  102.2 23.0 %collective-permute-start.5 = (f32[4,129,128]{2,0,1:T(4,128)S(1)}, f32[4,129,128]{2,0,1:T(4,128)S(1)}, u32[]{:S(2)}, u32[]{:S(2)}) collective-permute-start(f32[4,129,128]{2,0,1:T(4,128)S(1)} %copy.47), channel_id=1, source_target_pairs={{0,1},{1,0},{2,3},{3,2},{4,5},{5,4},{6,7},{7,6},{8,9},{9,8},{10,11... | collective-permute-start | bytes 792584 | tf_op jit(solution)/shard_map/ppermute | solution.py:129
  112.3 15.6 %copy-start.4 = (f32[544,128]{1,0:T(8,128)S(1)}, f32[544,128]{1,0:T(8,128)}, u32[]{:S(2)}) copy-start(f32[544,128]{1,0:T(8,128)} %shard_map.47) | copy-start | bytes 835588
  113.4 14.5 %collective-permute-start.12 = (f32[4,129,128]{2,0,1:T(4,128)S(1)}, f32[4,129,128]{2,0,1:T(4,128)S(1)}, u32[]{:S(2)}, u32[]{:S(2)}) collective-permute-start(f32[4,129,128]{2,0,1:T(4,128)S(1)} %copy.48), channel_id=1, source_target_pairs={{0,1},{1,0},{2,3},{3,2},{4,5},{5,4},{6,7},{7,6},{8,9},{9,8},{10,11... | collective-permute-start | bytes 792584 | tf_op jit(solution)/shard_map/ppermute | solution.py:129
  123.5 12.2 %collective-permute-start.19 = (f32[4,129,128]{2,0,1:T(4,128)S(1)}, f32[4,129,128]{2,0,1:T(4,128)S(1)}, u32[]{:S(2)}, u32[]{:S(2)}) collective-permute-start(f32[4,129,128]{2,0,1:T(4,128)S(1)} %copy.49), channel_id=1, source_target_pairs={{0,1},{1,0},{2,3},{3,2},{4,5},{5,4},{6,7},{7,6},{8,9},{9,8},{10,11... | collective-permute-start | bytes 792584 | tf_op jit(solution)/shard_map/ppermute | solution.py:129
  125.3 27.2 %collective-permute-start.6 = (f32[4,129,128]{2,0,1:T(4,128)S(1)}, f32[4,129,128]{2,0,1:T(4,128)S(1)}, u32[]{:S(2)}, u32[]{:S(2)}) collective-permute-start(f32[4,129,128]{2,0,1:T(4,128)S(1)} %copy_add_fusion), channel_id=1, source_target_pairs={{0,2},{1,3},{2,0},{3,1},{4,6},{5,7},{6,4},{7,5},{8,10},{9,11},{10,... | collective-permute-start | bytes 792584 | tf_op jit(solution)/shard_map/ppermute | solution.py:129
  128.0 30.1 %collective-permute-start.13 = (f32[4,129,128]{2,0,1:T(4,128)S(1)}, f32[4,129,128]{2,0,1:T(4,128)S(1)}, u32[]{:S(2)}, u32[]{:S(2)}) collective-permute-start(f32[4,129,128]{2,0,1:T(4,128)S(1)} %copy_add_fusion.1), channel_id=1, source_target_pairs={{0,2},{1,3},{2,0},{3,1},{4,6},{5,7},{6,4},{7,5},{8,10},{9,11},{10,... | collective-permute-start | bytes 792584 | tf_op jit(solution)/shard_map/ppermute | solution.py:129
  136.8 24.3 %collective-permute-start.20 = (f32[4,129,128]{2,0,1:T(4,128)S(1)}, f32[4,129,128]{2,0,1:T(4,128)S(1)}, u32[]{:S(2)}, u32[]{:S(2)}) collective-permute-start(f32[4,129,128]{2,0,1:T(4,128)S(1)} %copy_add_fusion.2), channel_id=1, source_target_pairs={{0,2},{1,3},{2,0},{3,1},{4,6},{5,7},{6,4},{7,5},{8,10},{9,11},{10,... | collective-permute-start | bytes 792584 | tf_op jit(solution)/shard_map/ppermute | solution.py:129

commit v2 on v1

--- a/solution.py
+++ b/solution.py
@@ -104,6 +104,11 @@
         out_shape=jax.ShapeDtypeStruct((k_count * rows, chans), jnp.float32),
         scratch_shapes=[pltpu.VMEM((k_count * rows, nb * lanes), jnp.bfloat16)],
         compiler_params=pltpu.CompilerParams(dimension_semantics=("arbitrary",)),
+        cost_estimate=pl.CostEstimate(
+            flops=2 * k_count * rows * samples * chans,
+            bytes_accessed=2 * chans * samples + 4 * k_count * (samples + rows * chans),
+            transcendentals=0,
+        ),
     )(whitened, padded)
     return out.reshape(k_count, rows, chans)[:, : 2 * LAG + 1, :]
 
@@ -143,13 +148,38 @@
     ).astype(jnp.bfloat16)
     normalizer = 1.0 / math.sqrt(samples * lax.axis_size("win"))
 
+    def prepare(piece, section):
+        whitened = whiten(time_filter(chan_filter(piece, chan_table), time_table))
+        term = jnp.dot(selector[section], whitened, preferred_element_type=jnp.float32)
+        return whitened, xor_sum(term.astype(jnp.bfloat16), "chan")
+
+    pieces = [record[section] for section in range(count_steps)]
     results = []
+    pending = prepare(pieces[0], 0)
     for section in range(count_steps):
-        whitened = whiten(time_filter(chan_filter(record[section], chan_table), time_table))
-        term = jnp.dot(selector[section], whitened, preferred_element_type=jnp.float32)
-        panel = xor_sum(term.astype(jnp.bfloat16), "chan")
-        partial_corr = correlate_kernel(whitened, panel)
-        results.append(xor_sum(partial_corr, "win"))
+        upcoming = None
+        if section + 1 < count_steps:
+            upcoming = prepare(pieces[section + 1], section + 1)
+        whitened, panel = pending
+        if section >= 2:
+            whitened, panel, results[section - 2] = lax.optimization_barrier(
+                (whitened, panel, results[section - 2])
+            )
+        if section + 1 < count_steps:
+            partial_corr = correlate_kernel(whitened, panel)
+            if section + 2 < count_steps:
+                pieces[section + 2], partial_corr = lax.optimization_barrier(
+                    (pieces[section + 2], partial_corr)
+                )
+            results.append(xor_sum(partial_corr, "win"))
+        else:
+            half = panel.shape[0] // 2
+            parts = [
+                xor_sum(correlate_kernel(whitened, panel[:half]), "win"),
+                xor_sum(correlate_kernel(whitened, panel[half:]), "win"),
+            ]
+            results.append(jnp.concatenate(parts, axis=0))
+        pending = upcoming
     return jnp.stack(results) * normalizer
 
 

time: 163 us -> 163 us (level)
  waiting for transfers between devices: 30.9 us -> 21.5 us
  Pallas kernels: 23.2 us -> 28.8 us
  starting transfers between devices: 35 us -> 38.7 us
    ppermute x15 -> x17, waiting for transfers between devices: 30.9 us -> 21.5 us  [xor_sum(): x = x + lax.ppermute(x, axis, [(i, i ^ step) for i in range(count)])]
    ppermute x15 -> x17, starting transfers between devices: 18.4 us -> 25.1 us  [xor_sum(): x = x + lax.ppermute(x, axis, [(i, i ^ step) for i in range(count)])]
    pallas_call x3 -> x4, Pallas kernels: 23.2 us -> 28.8 us  [correlate_kernel(): pl.pallas_call(functools.partial(corr_body, nb, rows), grid=(grid,), in_s...]
    ppermute x3, starting transfers between devices: 12.7 us -> 9.57 us  [padded_2(): lax.ppermute(tail, axis, [(i, (i + 1) % count) for i in range(ends)])]
    unnamed x25 -> x23, local copies, waits for them, and re-layouts: 5.62 us -> 4.56 us
  transfers between devices with their start and end apart: 21 -> 23, of which waited for: 4 -> 6; matrix products, arithmetic and copies ran while one was open for 41% -> 37% of each run, Pallas kernels for 14% -> 18%
where the time goes in v2:
time: 163 us; the launch traced here: 162 us
  starting transfers between devices  38.7 us (24%)
  local copies, waits for them, and re-layouts  35.5 us (22%)
  Pallas kernels  28.8 us (18%)
  other arithmetic  21.7 us (13%)
  waiting for transfers between devices  21.5 us (13%)
  matrix products  15.2 us (9%)
    pallas_call x4, Pallas kernels, correlate_kernel(): pl.pallas_call(functools.partial(corr_body, nb, rows), grid=(grid,), in_s...  28.8 us
    ppermute x17, starting transfers between devices, xor_sum(): x = x + lax.ppermute(x, axis, [(i, i ^ step) for i in range(count)])  25.1 us
    ppermute x17, waiting for transfers between devices, xor_sum(): x = x + lax.ppermute(x, axis, [(i, i ^ step) for i in range(count)])  21.5 us
    reshape x3, local copies, waits for them, and re-layouts, time_filter(): return result.reshape(channels_here, samples)  16.9 us
    convert_element_type x6, other arithmetic, whiten(): return (time_pass * lax.rsqrt(power + 1e-06)).astype(jnp.bfloat16)  13.3 us
    ppermute x3, starting transfers between devices, padded_2(): lax.ppermute(tail, axis, [(i, (i + 1) % count) for i in range(ends)])  9.57 us
    dot_general x3, matrix products, time_filter(): jnp.einsum('cbr,rt->cbt', extended, weights, preferred_element_type=jnp.f...  7.93 us
    squeeze x1, local copies, waits for them, and re-layouts, body(): pieces = [record[section] for section in range(count_steps)]  5.46 us
  transfers between devices with their start and end apart: 23, of which 6 were waited for; matrix products, arithmetic and copies ran while one was open for 37% of the time, Pallas kernels for 18%

profile of v2, /device:TPU:0, one launch (start us, length us, event | category | flops | bytes accessed | tf_op | source)
XLA Modules:
  0.0 161.9 jit_solution(3624829306374908917)
XLA Ops:
  1.3 3.1 %collective-permute-start.12 = (bf16[16,8192]{1,0:T(8,128)(2,1)S(1)}, bf16[16,8192]{1,0:T(8,128)(2,1)}, u32[]{:S(2)}, u32[]{:S(2)}) collective-permute-start(bf16[16,8192]{1,0:T(8,128)(2,1)S(1)} %get-tuple-element.15), channel_id=1, source_target_pairs={{0,4},{4,8},{8,12},{12,16},{16,20},{20,24},{24,28},{1,5},{5,9},{9,... | collective-permute-start | bytes 786440 | tf_op jit(solution)/shard_map/ppermute | solution.py:22
  5.7 5.1 %collective-permute-start = (bf16[16,8192]{1,0:T(8,128)(2,1)S(1)}, bf16[16,8192]{1,0:T(8,128)(2,1)}, u32[]{:S(2)}, u32[]{:S(2)}) collective-permute-start(bf16[16,8192]{1,0:T(8,128)(2,1)S(1)} %get-tuple-element.17), channel_id=1, source_target_pairs={{0,4},{4,8},{8,12},{12,16},{16,20},{20,24},{24,28},{1,5},{5,9},{9,... | collective-permute-start | bytes 786440 | tf_op jit(solution)/shard_map/ppermute | solution.py:22
  12.2 5.5 %slice_bitcast_fusion = (bf16[128,8192]{1,0:T(8,128)(2,1)}, bf16[128,8192]{1,0:T(8,128)(2,1)}, bf16[128,8192]{1,0:T(8,128)(2,1)S(1)}) fusion(bf16[3,128,8192]{2,1,0:T(8,128)(2,1)} %param.4), kind=kLoop, calls=%fused_computation.72 | loop fusion | bytes 12582912 | tf_op jit(solution)/shard_map/squeeze | solution.py:156
  19.8 2.4 %fusion.60 = bf16[16,64,8,128]{3,2,1,0:T(8,128)(2,1)S(1)} fusion(bf16[16,8192]{1,0:T(8,128)(2,1)} %collective-permute-done.13, bf16[128,8192]{1,0:T(8,128)(2,1)} %get-tuple-element.19, bf16[16,8192]{1,0:T(8,128)(2,1)} %collective-permute-done.12, bf16[128,160]{0,1:T(8,128)(2,1)S(1)} %select_reduce_fusion.1), kind=kOutput, calls=%fused_computation.77 | convolution fusion | flops 344457216 | bytes 4759552 | tf_op jit(solution)/shard_map/dot_general | solution.py:120
  22.8 1.5 fusion.87
  24.3 2.6 %multiply_reduce_fusion = (f32[128]{0:T(128)S(1)}, f32[128,64,128]{0,2,1:T(8,128)S(1)}) fusion(bf16[384,128]{1,0:T(8,128)(2,1)S(1)} %select_reduce_fusion, bf16[128,63,128]{2,0,1:T(8,128)(2,1)S(1)} %get-tuple-element.23, bf16[128,63,128]{2,0,1:T(8,128)(2,1)S(1)} %get-tuple-element.22, bf16[128,64,128]{2,0,1:T(8,128)(2,1)S(1)} %bitcast.81), kind=kOutput, calls=%fused_computation.42 | convolution fusion | flops 838860672 | bytes 10519040 | tf_op jit(solution)/shard_map/cbr,rt->cbt/dot_general | solution.py:53
  27.0 2.1 %fusion.54 = bf16[16,64,8,128]{3,2,1,0:T(8,128)(2,1)S(1)} fusion(bf16[16,8192]{1,0:T(8,128)(2,1)} %collective-permute-done.1, bf16[128,8192]{1,0:T(8,128)(2,1)S(1)} %copy-done.3, bf16[16,8192]{1,0:T(8,128)(2,1)} %collective-permute-done, bf16[128,160]{0,1:T(8,128)(2,1)S(1)} %select_reduce_fusion.1), kind=kOutput, calls=%fused_computation.75 | convolution fusion | flops 344457216 | bytes 4759552 | tf_op jit(solution)/shard_map/dot_general | solution.py:120
  31.2 2.7 %multiply_reduce_fusion.2 = (f32[128]{0:T(128)S(1)}, f32[128,64,128]{0,2,1:T(8,128)S(1)}) fusion(bf16[384,128]{1,0:T(8,128)(2,1)S(1)} %select_reduce_fusion, bf16[128,63,128]{2,0,1:T(8,128)(2,1)S(1)} %get-tuple-element.29, bf16[128,63,128]{2,0,1:T(8,128)(2,1)S(1)} %get-tuple-element.28, bf16[128,64,128]{2,0,1:T(8,128)(2,1)S(1)} %bitcast.83), kind=kOutput, calls=%fused_computation.48 | convolution fusion | flops 838860672 | bytes 10519040 | tf_op jit(solution)/shard_map/cbr,rt->cbt/dot_general | solution.py:53
  35.8 1.7 %collective-permute-start.2 = (bf16[4,8192]{1,0:T(4,128)(2,1)S(1)}, bf16[4,8192]{1,0:T(4,128)(2,1)S(1)}, u32[]{:S(2)}, u32[]{:S(2)}) collective-permute-start(bf16[4,8192]{1,0:T(4,128)(2,1)S(1)} %convolution_convert_fusion.5), channel_id=1, source_target_pairs={{0,4},{4,0},{8,12},{12,8},{16,20},{20,16},{24,28},{28,24},{1,5},{5... | collective-permute-start | bytes 196616 | tf_op jit(solution)/shard_map/ppermute | solution.py:134
  38.8 2.5 %collective-permute-start.3 = (bf16[4,8192]{1,0:T(4,128)(2,1)S(1)}, bf16[4,8192]{1,0:T(4,128)(2,1)S(1)}, u32[]{:S(2)}, u32[]{:S(2)}) collective-permute-start(bf16[4,8192]{1,0:T(4,128)(2,1)S(1)} %add.112), channel_id=1, source_target_pairs={{0,8},{4,12},{8,0},{12,4},{16,24},{20,28},{24,16},{28,20},{1,9},{5... | collective-permute-start | bytes 196616 | tf_op jit(solution)/shard_map/ppermute | solution.py:134
  41.3 5.6 %copy.44 = f32[128,8192]{1,0:T(8,128)} copy(f32[128,8192]{0,1:T(8,128)} %bitcast.86) | data formatting | bytes 8388608 | tf_op jit(solution)/shard_map/reshape | solution.py:54
  47.2 3.4 %collective-permute-start.4 = (bf16[4,8192]{1,0:T(4,128)(2,1)S(1)}, bf16[4,8192]{1,0:T(4,128)(2,1)S(1)}, u32[]{:S(2)}, u32[]{:S(2)}) collective-permute-start(bf16[4,8192]{1,0:T(4,128)(2,1)S(1)} %add.113), channel_id=1, source_target_pairs={{0,16},{4,20},{8,24},{12,28},{16,0},{20,4},{24,8},{28,12},{1,17},{... | collective-permute-start | bytes 196616 | tf_op jit(solution)/shard_map/ppermute | solution.py:134
  50.7 3.9 %multiply_convert_fusion.5.w_ref = bf16[128,8192]{1,0:T(8,128)(2,1)} fusion(f32[128,8192]{1,0:T(8,128)} %copy.44, f32[128]{0:T(128)S(1)} %add_rsqrt_fusion.2), kind=kLoop, calls=%fused_computation.47 | loop fusion | flops 2097152 | bytes 6291968 | tf_op jit(solution)/shard_map/convert_element_type | solution.py:59
  54.6 5.6 %copy.48 = f32[128,8192]{1,0:T(8,128)} copy(f32[128,8192]{0,1:T(8,128)} %bitcast.84) | data formatting | bytes 8388608 | tf_op jit(solution)/shard_map/reshape | solution.py:54
  61.2 7.7 %shard_map.46 = f32[544,128]{1,0:T(8,128)} custom-call(bf16[128,8192]{1,0:T(8,128)(2,1)} %multiply_convert_fusion.5.w_ref, f32[4,8320]{1,0:T(4,128)} %pad_convert_fusion.1.p_ref), custom_call_target="tpu_custom_call" | custom-call | flops 1140850688 | bytes 2506752 | tf_op jit(solution)/shard_map/pallas_call | solution.py:96
  72.6 3.9 %multiply_convert_fusion.1.w_ref = bf16[128,8192]{1,0:T(8,128)(2,1)} fusion(f32[128,8192]{1,0:T(8,128)} %copy.48, f32[128]{0:T(128)S(1)} %add_rsqrt_fusion), kind=kLoop, calls=%fused_computation.41 | loop fusion | flops 2097152 | bytes 6291968 | tf_op jit(solution)/shard_map/convert_element_type | solution.py:59
  76.5 1.6 collective-permute-start.10
  81.0 2.7 %multiply_reduce_fusion.1 = (f32[128]{0:T(128)S(1)}, f32[128,64,128]{0,2,1:T(8,128)S(1)}) fusion(bf16[384,128]{1,0:T(8,128)(2,1)S(1)} %select_reduce_fusion, bf16[128,63,128]{2,0,1:T(8,128)(2,1)S(1)} %get-tuple-element.25, bf16[128,63,128]{2,0,1:T(8,128)(2,1)S(1)} %get-tuple-element.24, bf16[128,64,128]{2,0,1:T(8,128)(2,1)S(1)} %bitcast.79), kind=kOutput, calls=%fused_computation.45 | convolution fusion | flops 838860672 | bytes 10519040 | tf_op jit(solution)/shard_map/cbr,rt->cbt/dot_general | solution.py:53
  85.6 3.9 %collective-permute-start.7 = (bf16[4,8192]{1,0:T(4,128)(2,1)S(1)}, bf16[4,8192]{1,0:T(4,128)(2,1)S(1)}, u32[]{:S(2)}, u32[]{:S(2)}) collective-permute-start(bf16[4,8192]{1,0:T(4,128)(2,1)S(1)} %convolution_convert_fusion.4), channel_id=1, source_target_pairs={{0,4},{4,0},{8,12},{12,8},{16,20},{20,16},{24,28},{28,24},{1,5},{5... | collective-permute-start | bytes 196616 | tf_op jit(solution)/shard_map/ppermute | solution.py:134
  90.4 2.1 %collective-permute-start.8 = (bf16[4,8192]{1,0:T(4,128)(2,1)S(1)}, bf16[4,8192]{1,0:T(4,128)(2,1)S(1)}, u32[]{:S(2)}, u32[]{:S(2)}) collective-permute-start(bf16[4,8192]{1,0:T(4,128)(2,1)S(1)} %add.116), channel_id=1, source_target_pairs={{0,8},{4,12},{8,0},{12,4},{16,24},{20,28},{24,16},{28,20},{1,9},{5... | collective-permute-start | bytes 196616 | tf_op jit(solution)/shard_map/ppermute | solution.py:134
  92.5 7.7 %shard_map.47 = f32[544,128]{1,0:T(8,128)} custom-call(bf16[128,8192]{1,0:T(8,128)(2,1)} %multiply_convert_fusion.1.w_ref, f32[4,8320]{1,0:T(4,128)} %pad_convert_fusion.p_ref), custom_call_target="tpu_custom_call" | custom-call | flops 1140850688 | bytes 2506752 | tf_op jit(solution)/shard_map/pallas_call | solution.py:96
  101.3 1.6 %collective-permute-start.17 = (f32[4,129,128]{2,0,1:T(4,128)S(1)}, f32[4,129,128]{2,0,1:T(4,128)S(1)}, u32[]{:S(2)}, u32[]{:S(2)}) collective-permute-start(f32[4,129,128]{2,0,1:T(4,128)S(1)} %copy.50), channel_id=1, source_target_pairs={{0,1},{1,0},{2,3},{3,2},{4,5},{5,4},{6,7},{7,6},{8,9},{9,8},{10,11... | collective-permute-start | bytes 792584 | tf_op jit(solution)/shard_map/ppermute | solution.py:134
  102.9 5.6 %copy.46 = f32[128,8192]{1,0:T(8,128)} copy(f32[128,8192]{0,1:T(8,128)} %bitcast.85) | data formatting | bytes 8388608 | tf_op jit(solution)/shard_map/reshape | solution.py:54
  108.6 2.7 %collective-permute-start.11 = (f32[4,129,128]{2,0,1:T(4,128)S(1)}, f32[4,129,128]{2,0,1:T(4,128)S(1)}, u32[]{:S(2)}, u32[]{:S(2)}) collective-permute-start(f32[4,129,128]{2,0,1:T(4,128)S(1)} %add.119), channel_id=1, source_target_pairs={{0,2},{1,3},{2,0},{3,1},{4,6},{5,7},{6,4},{7,5},{8,10},{9,11},{10,... | collective-permute-start | bytes 792584 | tf_op jit(solution)/shard_map/ppermute | solution.py:134
  111.4 3.9 %multiply_convert_fusion.3.w_ref = bf16[128,8192]{1,0:T(8,128)(2,1)} fusion(f32[128,8192]{1,0:T(8,128)} %copy.46, f32[128]{0:T(128)S(1)} %add_rsqrt_fusion.1), kind=kLoop, calls=%fused_computation.44 | loop fusion | flops 2097152 | bytes 6291968 | tf_op jit(solution)/shard_map/convert_element_type | solution.py:59
  115.7 7.5 %collective-permute-done.11 = f32[4,129,128]{2,0,1:T(4,128)S(1)} collective-permute-done((f32[4,129,128]{2,0,1:T(4,128)S(1)}, f32[4,129,128]{2,0,1:T(4,128)S(1)}, u32[]{:S(2)}, u32[]{:S(2)}) %collective-permute-start.11) | collective-permute-done | bytes 264224 | tf_op jit(solution)/shard_map/ppermute | solution.py:134
  124.1 6.7 %shard_map.48 = f32[272,128]{1,0:T(8,128)} custom-call(bf16[128,8192]{1,0:T(8,128)(2,1)} %multiply_convert_fusion.3.w_ref, f32[2,8320]{1,0:T(2,128)} %get-tuple-element.39.p_ref), custom_call_target="tpu_custom_call" | custom-call | flops 570425344 | bytes 2301952 | tf_op jit(solution)/shard_map/pallas_call | solution.py:96
  132.0 3.2 %collective-permute-start.18 = (f32[4,129,128]{2,0,1:T(4,128)S(1)}, f32[4,129,128]{2,0,1:T(4,128)S(1)}, u32[]{:S(2)}, u32[]{:S(2)}) collective-permute-start(f32[4,129,128]{2,0,1:T(4,128)S(1)} %copy_add_fusion), channel_id=1, source_target_pairs={{0,2},{1,3},{2,0},{3,1},{4,6},{5,7},{6,4},{7,5},{8,10},{9,11},{10,... | collective-permute-start | bytes 792584 | tf_op jit(solution)/shard_map/ppermute | solution.py:134
  135.1 6.7 %shard_map.49 = f32[272,128]{1,0:T(8,128)} custom-call(bf16[128,8192]{1,0:T(8,128)(2,1)} %multiply_convert_fusion.3.w_ref, f32[2,8320]{1,0:T(2,128)} %get-tuple-element.38.p_ref), custom_call_target="tpu_custom_call" | custom-call | flops 570425344 | bytes 2301952 | tf_op jit(solution)/shard_map/pallas_call | solution.py:96
  143.9 1.8 %collective-permute-start.20 = (f32[2,129,128]{2,0,1:T(2,128)S(1)}, f32[2,129,128]{2,0,1:T(2,128)S(1)}, u32[]{:S(2)}, u32[]{:S(2)}) collective-permute-start(f32[2,129,128]{2,0,1:T(2,128)S(1)} %copy_add_fusion.1), channel_id=1, source_target_pairs={{0,2},{1,3},{2,0},{3,1},{4,6},{5,7},{6,4},{7,5},{8,10},{9,11},{10,... | collective-permute-start | bytes 396296 | tf_op jit(solution)/shard_map/ppermute | solution.py:134
  145.8 5.5 %collective-permute-done.21 = f32[2,129,128]{2,0,1:T(2,128)S(1)} collective-permute-done((f32[2,129,128]{2,0,1:T(2,128)S(1)}, f32[2,129,128]{2,0,1:T(2,128)S(1)}, u32[]{:S(2)}, u32[]{:S(2)}) %collective-permute-start.21) | collective-permute-done | bytes 132128 | tf_op jit(solution)/shard_map/ppermute | solution.py:134
  152.7 7.8 %collective-permute-done.22 = f32[2,129,128]{2,0,1:T(2,128)S(1)} collective-permute-done((f32[2,129,128]{2,0,1:T(2,128)S(1)}, f32[2,129,128]{2,0,1:T(2,128)S(1)}, u32[]{:S(2)}, u32[]{:S(2)}) %collective-permute-start.22) | collective-permute-done | bytes 132128 | tf_op jit(solution)/shard_map/ppermute | solution.py:134
  (104 shorter events, 30.9 us)
Async XLA Ops:
  1.3 18.5 %collective-permute-start.12 = (bf16[16,8192]{1,0:T(8,128)(2,1)S(1)}, bf16[16,8192]{1,0:T(8,128)(2,1)}, u32[]{:S(2)}, u32[]{:S(2)}) collective-permute-start(bf16[16,8192]{1,0:T(8,128)(2,1)S(1)} %get-tuple-element.15), channel_id=1, source_target_pairs={{0,4},{4,8},{8,12},{12,16},{16,20},{20,24},{24,28},{1,5},{5,9},{9,... | collective-permute-start | bytes 786440 | tf_op jit(solution)/shard_map/ppermute | solution.py:22
  4.4 15.4 %collective-permute-start.13 = (bf16[16,8192]{1,0:T(8,128)(2,1)S(1)}, bf16[16,8192]{1,0:T(8,128)(2,1)}, u32[]{:S(2)}, u32[]{:S(2)}) collective-permute-start(bf16[16,8192]{1,0:T(8,128)(2,1)S(1)} %get-tuple-element.18), channel_id=1, source_target_pairs={{4,0},{8,4},{12,8},{16,12},{20,16},{24,20},{28,24},{5,1},{9,5},{13... | collective-permute-start | bytes 786440 | tf_op jit(solution)/shard_map/ppermute | solution.py:24
  5.7 21.3 %collective-permute-start = (bf16[16,8192]{1,0:T(8,128)(2,1)S(1)}, bf16[16,8192]{1,0:T(8,128)(2,1)}, u32[]{:S(2)}, u32[]{:S(2)}) collective-permute-start(bf16[16,8192]{1,0:T(8,128)(2,1)S(1)} %get-tuple-element.17), channel_id=1, source_target_pairs={{0,4},{4,8},{8,12},{12,16},{16,20},{20,24},{24,28},{1,5},{5,9},{9,... | collective-permute-start | bytes 786440 | tf_op jit(solution)/shard_map/ppermute | solution.py:22
  10.8 6.9 %copy-start.8 = (f32[33]{0:T(128)S(1)}, f32[33]{0:T(128)}, u32[]{:S(2)}) copy-start(f32[33]{0:T(128)} %param.5) | copy-start | bytes 400
  10.8 7.1 %copy-start.9 = (f32[65]{0:T(128)S(1)}, f32[65]{0:T(128)}, u32[]{:S(2)}) copy-start(f32[65]{0:T(128)} %param.6) | copy-start | bytes 784
  10.8 8.5 %copy-start.7 = (s32[3,4]{1,0:T(4,128)S(1)}, s32[3,4]{1,0:T(4,128)}, u32[]{:S(2)}) copy-start(s32[3,4]{1,0:T(4,128)} %param.7) | copy-start | bytes 148
  10.8 16.1 %collective-permute-start.1 = (bf16[16,8192]{1,0:T(8,128)(2,1)S(1)}, bf16[16,8192]{1,0:T(8,128)(2,1)}, u32[]{:S(2)}, u32[]{:S(2)}) collective-permute-start(bf16[16,8192]{1,0:T(8,128)(2,1)S(1)} %get-tuple-element.16), channel_id=1, source_target_pairs={{4,0},{8,4},{12,8},{16,12},{20,16},{24,20},{28,24},{5,1},{9,5},{13... | collective-permute-start | bytes 786440 | tf_op jit(solution)/shard_map/ppermute | solution.py:24
  19.7 7.3 %copy-start.5 = (bf16[128,160]{0,1:T(8,128)(2,1)}, bf16[128,160]{0,1:T(8,128)(2,1)S(1)}, u32[]{:S(2)}) copy-start(bf16[128,160]{0,1:T(8,128)(2,1)S(1)} %select_reduce_fusion.1) | copy-start | bytes 122884
  24.3 2.7 %copy-start.3 = (bf16[128,8192]{1,0:T(8,128)(2,1)S(1)}, bf16[128,8192]{1,0:T(8,128)(2,1)}, u32[]{:S(2)}) copy-start(bf16[128,8192]{1,0:T(8,128)(2,1)} %get-tuple-element.20) | copy-start | bytes 6291460
  26.9 10.6 %copy-start = (f32[128,64,128]{0,2,1:T(8,128)}, f32[128,64,128]{0,2,1:T(8,128)S(1)}, u32[]{:S(2)}) copy-start(f32[128,64,128]{0,2,1:T(8,128)S(1)} %get-tuple-element.37) | copy-start | bytes 12582916
  33.9 2.0 %copy-start.2 = (f32[128,64,128]{0,2,1:T(8,128)}, f32[128,64,128]{0,2,1:T(8,128)S(1)}, u32[]{:S(2)}) copy-start(f32[128,64,128]{0,2,1:T(8,128)S(1)} %get-tuple-element.33) | copy-start | bytes 12582916
  35.8 2.9 %collective-permute-start.2 = (bf16[4,8192]{1,0:T(4,128)(2,1)S(1)}, bf16[4,8192]{1,0:T(4,128)(2,1)S(1)}, u32[]{:S(2)}, u32[]{:S(2)}) collective-permute-start(bf16[4,8192]{1,0:T(4,128)(2,1)S(1)} %convolution_convert_fusion.5), channel_id=1, source_target_pairs={{0,4},{4,0},{8,12},{12,8},{16,20},{20,16},{24,28},{28,24},{1,5},{5... | collective-permute-start | bytes 196616 | tf_op jit(solution)/shard_map/ppermute | solution.py:134
  38.7 8.2 %collective-permute-start.14 = (bf16[4,8192]{1,0:T(4,128)(2,1)S(1)}, bf16[4,8192]{1,0:T(4,128)(2,1)S(1)}, u32[]{:S(2)}, u32[]{:S(2)}) collective-permute-start(bf16[4,8192]{1,0:T(4,128)(2,1)S(1)} %convolution_convert_fusion.3), channel_id=1, source_target_pairs={{0,4},{4,0},{8,12},{12,8},{16,20},{20,16},{24,28},{28,24},{1,5},{5... | collective-permute-start | bytes 196616 | tf_op jit(solution)/shard_map/ppermute | solution.py:134
  38.8 8.4 %collective-permute-start.3 = (bf16[4,8192]{1,0:T(4,128)(2,1)S(1)}, bf16[4,8192]{1,0:T(4,128)(2,1)S(1)}, u32[]{:S(2)}, u32[]{:S(2)}) collective-permute-start(bf16[4,8192]{1,0:T(4,128)(2,1)S(1)} %add.112), channel_id=1, source_target_pairs={{0,8},{4,12},{8,0},{12,4},{16,24},{20,28},{24,16},{28,20},{1,9},{5... | collective-permute-start | bytes 196616 | tf_op jit(solution)/shard_map/ppermute | solution.py:134
  46.9 13.3 %collective-permute-start.15 = (bf16[4,8192]{1,0:T(4,128)(2,1)S(1)}, bf16[4,8192]{1,0:T(4,128)(2,1)S(1)}, u32[]{:S(2)}, u32[]{:S(2)}) collective-permute-start(bf16[4,8192]{1,0:T(4,128)(2,1)S(1)} %add.122), channel_id=1, source_target_pairs={{0,8},{4,12},{8,0},{12,4},{16,24},{20,28},{24,16},{28,20},{1,9},{5... | collective-permute-start | bytes 196616 | tf_op jit(solution)/shard_map/ppermute | solution.py:134
  47.2 13.1 %collective-permute-start.4 = (bf16[4,8192]{1,0:T(4,128)(2,1)S(1)}, bf16[4,8192]{1,0:T(4,128)(2,1)S(1)}, u32[]{:S(2)}, u32[]{:S(2)}) collective-permute-start(bf16[4,8192]{1,0:T(4,128)(2,1)S(1)} %add.113), channel_id=1, source_target_pairs={{0,16},{4,20},{8,24},{12,28},{16,0},{20,4},{24,8},{28,12},{1,17},{... | collective-permute-start | bytes 196616 | tf_op jit(solution)/shard_map/ppermute | solution.py:134
  60.3 17.8 %collective-permute-start.16 = (bf16[4,8192]{1,0:T(4,128)(2,1)S(1)}, bf16[4,8192]{1,0:T(4,128)(2,1)S(1)}, u32[]{:S(2)}, u32[]{:S(2)}) collective-permute-start(bf16[4,8192]{1,0:T(4,128)(2,1)S(1)} %add.123), channel_id=1, source_target_pairs={{0,16},{4,20},{8,24},{12,28},{16,0},{20,4},{24,8},{28,12},{1,17},{... | collective-permute-start | bytes 196616 | tf_op jit(solution)/shard_map/ppermute | solution.py:134
  68.9 9.3 %copy-start.6 = (bf16[128,160]{0,1:T(8,128)(2,1)S(1)}, bf16[128,160]{0,1:T(8,128)(2,1)}, u32[]{:S(2)}) copy-start(bf16[128,160]{0,1:T(8,128)(2,1)} %copy-done.5) | copy-start | bytes 122884
  70.0 8.2 %collective-permute-start.5 = (bf16[16,8192]{1,0:T(8,128)(2,1)S(1)}, bf16[16,8192]{1,0:T(8,128)(2,1)S(1)}, u32[]{:S(2)}, u32[]{:S(2)}) collective-permute-start(bf16[16,8192]{1,0:T(8,128)(2,1)S(1)} %get-tuple-element.26), channel_id=1, source_target_pairs={{0,4},{4,8},{8,12},{12,16},{16,20},{20,24},{24,28},{1,5},{5,9},{9,... | collective-permute-start | bytes 786440 | tf_op jit(solution)/shard_map/ppermute | solution.py:22
  71.3 6.9 %collective-permute-start.6 = (bf16[16,8192]{1,0:T(8,128)(2,1)S(1)}, bf16[16,8192]{1,0:T(8,128)(2,1)S(1)}, u32[]{:S(2)}, u32[]{:S(2)}) collective-permute-start(bf16[16,8192]{1,0:T(8,128)(2,1)S(1)} %get-tuple-element.27), channel_id=1, source_target_pairs={{4,0},{8,4},{12,8},{16,12},{20,16},{24,20},{28,24},{5,1},{9,5},{13... | collective-permute-start | bytes 786440 | tf_op jit(solution)/shard_map/ppermute | solution.py:24
  76.5 32.0 %collective-permute-start.10 = (f32[4,129,128]{2,0,1:T(4,128)S(1)}, f32[4,129,128]{2,0,1:T(4,128)S(1)}, u32[]{:S(2)}, u32[]{:S(2)}) collective-permute-start(f32[4,129,128]{2,0,1:T(4,128)S(1)} %copy.49), channel_id=1, source_target_pairs={{0,1},{1,0},{2,3},{3,2},{4,5},{5,4},{6,7},{7,6},{8,9},{9,8},{10,11... | collective-permute-start | bytes 792584 | tf_op jit(solution)/shard_map/ppermute | solution.py:134
  85.6 4.8 %collective-permute-start.7 = (bf16[4,8192]{1,0:T(4,128)(2,1)S(1)}, bf16[4,8192]{1,0:T(4,128)(2,1)S(1)}, u32[]{:S(2)}, u32[]{:S(2)}) collective-permute-start(bf16[4,8192]{1,0:T(4,128)(2,1)S(1)} %convolution_convert_fusion.4), channel_id=1, source_target_pairs={{0,4},{4,0},{8,12},{12,8},{16,20},{20,16},{24,28},{28,24},{1,5},{5... | collective-permute-start | bytes 196616 | tf_op jit(solution)/shard_map/ppermute | solution.py:134
  90.4 20.8 %collective-permute-start.8 = (bf16[4,8192]{1,0:T(4,128)(2,1)S(1)}, bf16[4,8192]{1,0:T(4,128)(2,1)S(1)}, u32[]{:S(2)}, u32[]{:S(2)}) collective-permute-start(bf16[4,8192]{1,0:T(4,128)(2,1)S(1)} %add.116), channel_id=1, source_target_pairs={{0,8},{4,12},{8,0},{12,4},{16,24},{20,28},{24,16},{28,20},{1,9},{5... | collective-permute-start | bytes 196616 | tf_op jit(solution)/shard_map/ppermute | solution.py:134
  101.3 30.6 %collective-permute-start.17 = (f32[4,129,128]{2,0,1:T(4,128)S(1)}, f32[4,129,128]{2,0,1:T(4,128)S(1)}, u32[]{:S(2)}, u32[]{:S(2)}) collective-permute-start(f32[4,129,128]{2,0,1:T(4,128)S(1)} %copy.50), channel_id=1, source_target_pairs={{0,1},{1,0},{2,3},{3,2},{4,5},{5,4},{6,7},{7,6},{8,9},{9,8},{10,11... | collective-permute-start | bytes 792584 | tf_op jit(solution)/shard_map/ppermute | solution.py:134
  108.6 14.6 %collective-permute-start.11 = (f32[4,129,128]{2,0,1:T(4,128)S(1)}, f32[4,129,128]{2,0,1:T(4,128)S(1)}, u32[]{:S(2)}, u32[]{:S(2)}) collective-permute-start(f32[4,129,128]{2,0,1:T(4,128)S(1)} %add.119), channel_id=1, source_target_pairs={{0,2},{1,3},{2,0},{3,1},{4,6},{5,7},{6,4},{7,5},{8,10},{9,11},{10,... | collective-permute-start | bytes 792584 | tf_op jit(solution)/shard_map/ppermute | solution.py:134
  111.3 20.6 %copy-start.4 = (f32[544,128]{1,0:T(8,128)S(1)}, f32[544,128]{1,0:T(8,128)}, u32[]{:S(2)}) copy-start(f32[544,128]{1,0:T(8,128)} %shard_map.47) | copy-start | bytes 835588
  111.3 4.3 %collective-permute-start.9 = (bf16[4,8192]{1,0:T(4,128)(2,1)S(1)}, bf16[4,8192]{1,0:T(4,128)(2,1)S(1)}, u32[]{:S(2)}, u32[]{:S(2)}) collective-permute-start(bf16[4,8192]{1,0:T(4,128)(2,1)S(1)} %add.117), channel_id=1, source_target_pairs={{0,16},{4,20},{8,24},{12,28},{16,0},{20,4},{24,8},{28,12},{1,17},{... | collective-permute-start | bytes 196616 | tf_op jit(solution)/shard_map/ppermute | solution.py:134
  131.8 11.2 %collective-permute-start.19 = (f32[2,129,128]{2,0,1:T(2,128)S(1)}, f32[2,129,128]{2,0,1:T(2,128)S(1)}, u32[]{:S(2)}, u32[]{:S(2)}) collective-permute-start(f32[2,129,128]{2,0,1:T(2,128)S(1)} %copy.51), channel_id=1, source_target_pairs={{0,1},{1,0},{2,3},{3,2},{4,5},{5,4},{6,7},{7,6},{8,9},{9,8},{10,11... | collective-permute-start | bytes 396296 | tf_op jit(solution)/shard_map/ppermute | solution.py:134
  132.0 20.4 %collective-permute-start.18 = (f32[4,129,128]{2,0,1:T(4,128)S(1)}, f32[4,129,128]{2,0,1:T(4,128)S(1)}, u32[]{:S(2)}, u32[]{:S(2)}) collective-permute-start(f32[4,129,128]{2,0,1:T(4,128)S(1)} %copy_add_fusion), channel_id=1, source_target_pairs={{0,2},{1,3},{2,0},{3,1},{4,6},{5,7},{6,4},{7,5},{8,10},{9,11},{10,... | collective-permute-start | bytes 792584 | tf_op jit(solution)/shard_map/ppermute | solution.py:134
  142.8 8.5 %collective-permute-start.21 = (f32[2,129,128]{2,0,1:T(2,128)S(1)}, f32[2,129,128]{2,0,1:T(2,128)S(1)}, u32[]{:S(2)}, u32[]{:S(2)}) collective-permute-start(f32[2,129,128]{2,0,1:T(2,128)S(1)} %copy.52), channel_id=1, source_target_pairs={{0,1},{1,0},{2,3},{3,2},{4,5},{5,4},{6,7},{7,6},{8,9},{9,8},{10,11... | collective-permute-start | bytes 396296 | tf_op jit(solution)/shard_map/ppermute | solution.py:134
  143.9 8.7 %collective-permute-start.20 = (f32[2,129,128]{2,0,1:T(2,128)S(1)}, f32[2,129,128]{2,0,1:T(2,128)S(1)}, u32[]{:S(2)}, u32[]{:S(2)}) collective-permute-start(f32[2,129,128]{2,0,1:T(2,128)S(1)} %copy_add_fusion.1), channel_id=1, source_target_pairs={{0,2},{1,3},{2,0},{3,1},{4,6},{5,7},{6,4},{7,5},{8,10},{9,11},{10,... | collective-permute-start | bytes 396296 | tf_op jit(solution)/shard_map/ppermute | solution.py:134
  152.3 8.2 %collective-permute-start.22 = (f32[2,129,128]{2,0,1:T(2,128)S(1)}, f32[2,129,128]{2,0,1:T(2,128)S(1)}, u32[]{:S(2)}, u32[]{:S(2)}) collective-permute-start(f32[2,129,128]{2,0,1:T(2,128)S(1)} %copy_add_fusion.2), channel_id=1, source_target_pairs={{0,2},{1,3},{2,0},{3,1},{4,6},{5,7},{6,4},{7,5},{8,10},{9,11},{10,... | collective-permute-start | bytes 396296 | tf_op jit(solution)/shard_map/ppermute | solution.py:134
  (1 other events, 2.0 us)

commit v3 on v2

--- a/solution.py
+++ b/solution.py
@@ -125,6 +125,75 @@
     return total.astype(jnp.bfloat16)
 
 
+def prep_body(section_chunk, rec_ref, lo_ref, hi_ref, blo_ref, bmid_ref, bhi_ref, tw_ref, o_ref, cp_ref, tp_ref):
+    chans, samples = o_ref.shape
+    lanes = 128
+    cp_ref[:, pl.ds(0, lanes)] = jnp.zeros((chans, lanes), cp_ref.dtype)
+    cp_ref[:, pl.ds(samples + lanes, lanes)] = jnp.zeros((chans, lanes), cp_ref.dtype)
+    chunk = section_chunk
+
+    def chan_step(i, carry):
+        off = pl.multiple_of(i * chunk, chunk)
+        total = jnp.dot(bmid_ref[...], rec_ref[0, :, pl.ds(off, chunk)], preferred_element_type=jnp.float32)
+        total += jnp.dot(blo_ref[...], lo_ref[:, pl.ds(off, chunk)], preferred_element_type=jnp.float32)
+        total += jnp.dot(bhi_ref[...], hi_ref[:, pl.ds(off, chunk)], preferred_element_type=jnp.float32)
+        cp_ref[:, pl.ds(pl.multiple_of(off + lanes, lanes), chunk)] = total.astype(cp_ref.dtype)
+        return carry
+
+    lax.fori_loop(0, samples // chunk, chan_step, 0)
+
+    def time_step(b, acc):
+        off = pl.multiple_of(b * lanes, lanes)
+        y = jnp.dot(cp_ref[:, pl.ds(off, 3 * lanes)], tw_ref[...], preferred_element_type=jnp.float32)
+        tp_ref[:, pl.ds(off, lanes)] = y
+        return acc + y * y
+
+    acc = lax.fori_loop(0, samples // lanes, time_step, jnp.zeros((chans, lanes), jnp.float32))
+    power = jnp.sum(acc, axis=1, keepdims=True) / samples
+    scale = lax.rsqrt(power + 1e-06)
+
+    def white_step(i, carry):
+        off = pl.multiple_of(i * chunk, chunk)
+        o_ref[:, pl.ds(off, chunk)] = (tp_ref[:, pl.ds(off, chunk)] * scale).astype(o_ref.dtype)
+        return carry
+
+    lax.fori_loop(0, samples // chunk, white_step, 0)
+
+
+def prepare_kernel(record, section, lo, hi, band, time_weights):
+    count_steps, chans, samples = record.shape
+    half = lo.shape[0]
+    lanes = 128
+    chunk = 512
+    blo, bmid, bhi = band[:, :half], band[:, half:half + chans], band[:, half + chans:]
+    full = lambda i: (0, 0)
+    return pl.pallas_call(
+        functools.partial(prep_body, chunk),
+        grid=(1,),
+        in_specs=[
+            pl.BlockSpec((1, chans, samples), lambda i: (section, 0, 0)),
+            pl.BlockSpec((half, samples), full),
+            pl.BlockSpec((half, samples), full),
+            pl.BlockSpec((chans, half), full),
+            pl.BlockSpec((chans, chans), full),
+            pl.BlockSpec((chans, half), full),
+            pl.BlockSpec(time_weights.shape, full),
+        ],
+        out_specs=pl.BlockSpec((chans, samples), full),
+        out_shape=jax.ShapeDtypeStruct((chans, samples), jnp.bfloat16),
+        scratch_shapes=[
+            pltpu.VMEM((chans, samples + 2 * lanes), jnp.bfloat16),
+            pltpu.VMEM((chans, samples), jnp.float32),
+        ],
+        compiler_params=pltpu.CompilerParams(vmem_limit_bytes=48 * 1024 * 1024),
+        cost_estimate=pl.CostEstimate(
+            flops=2 * chans * samples * (chans + 2 * half + 3 * lanes),
+            bytes_accessed=2 * samples * (2 * chans + 2 * half),
+            transcendentals=chans,
+        ),
+    )(record, lo, hi, blo, bmid, bhi, time_weights)
+
+
 def xor_sum(x, axis):
     count = lax.axis_size(axis)
     if count & (count - 1):
@@ -148,12 +217,22 @@
     ).astype(jnp.bfloat16)
     normalizer = 1.0 / math.sqrt(samples * lax.axis_size("win"))
 
-    def prepare(piece, section):
-        whitened = whiten(time_filter(chan_filter(piece, chan_table), time_table))
+    half = (chan_table.shape[0] - 1) // 2
+    count = lax.axis_size("chan")
+    band = band_matrix(chan_table, channels_here, channels_here + 2 * half)
+    offset = lax.iota(jnp.int32, 384)[:, None] - 128 - lax.iota(jnp.int32, 128)[None, :]
+    time_weights = tap_lookup(offset + (time_table.shape[0] - 1) // 2, time_table)
+
+    def prepare(whole, section):
+        head = whole[section, :half]
+        tail = whole[section, channels_here - half :]
+        lower = lax.ppermute(tail, "chan", [(i, i + 1) for i in range(count - 1)])
+        upper = lax.ppermute(head, "chan", [(i + 1, i) for i in range(count - 1)])
+        whitened = prepare_kernel(whole, section, lower, upper, band, time_weights)
         term = jnp.dot(selector[section], whitened, preferred_element_type=jnp.float32)
         return whitened, xor_sum(term.astype(jnp.bfloat16), "chan")
 
-    pieces = [record[section] for section in range(count_steps)]
+    pieces = [record] * count_steps
     results = []
     pending = prepare(pieces[0], 0)
     for section in range(count_steps):

time: 163 us -> 162 us (level)
  Pallas kernels: 28.8 us -> 80.4 us
  local copies, waits for them, and re-layouts: 35.5 us -> 6.8 us
  matrix products: 15.2 us -> 1.15 us
  other arithmetic: 21.7 us -> 9.58 us
  waiting for transfers between devices: 21.5 us -> 24.3 us
    pallas_call x0 -> x3, Pallas kernels: none -> 51.6 us  [prepare_kernel(): pl.pallas_call(functools.partial(prep_body, chunk), grid=(1,), in_specs=[...]
    reshape x6 -> x0, local copies, waits for them, and re-layouts: 18.6 us -> none  [the longest x3 16.9 us: time_filter(): return result.reshape(channels_here, samples)]
    convert_element_type x6 -> x0, other arithmetic: 13.3 us -> none  [whiten(): return (time_pass * lax.rsqrt(power + 1e-06)).astype(jnp.bfloat16)]
    dot_general x6 -> x0, matrix products: 13.2 us -> none  [the longest x3 7.93 us: time_filter(): jnp.einsum('cbr,rt->cbt', extended, weights, preferred_element_type=jnp.f...]
    slice x5 -> x2, local copies, waits for them, and re-layouts: 5.74 us -> 0.16 us  [the longest x1 0.08 us: prepare_kernel(): band[:, half:half + chans]]
    squeeze x1 -> x2, local copies, waits for them, and re-layouts: 5.46 us -> 2.32 us  [prepare(): head = whole[section, :half]]
    ppermute x17, waiting for transfers between devices: 21.5 us -> 24.3 us  [xor_sum(): x = x + lax.ppermute(x, axis, [(i, i ^ step) for i in range(count)])]
    unnamed x23 -> x13, local copies, waits for them, and re-layouts: 4.56 us -> 3.14 us
  transfers between devices with their start and end apart: 23 -> 23, of which waited for: 6 -> 8; matrix products, arithmetic and copies ran while one was open for 37% -> 7% of each run, Pallas kernels for 18% -> 45%
where the time goes in v3:
time: 162 us; the launch traced here: 161 us
  Pallas kernels  80.4 us (50%)
  starting transfers between devices  38.7 us (24%)
  waiting for transfers between devices  24.3 us (15%)
  other arithmetic  9.58 us (6%)
  local copies, waits for them, and re-layouts  6.8 us (4%)
    pallas_call x3, Pallas kernels, prepare_kernel(): pl.pallas_call(functools.partial(prep_body, chunk), grid=(1,), in_specs=[...  51.6 us
    pallas_call x4, Pallas kernels, correlate_kernel(): pl.pallas_call(functools.partial(corr_body, nb, rows), grid=(grid,), in_s...  28.8 us
    ppermute x17, starting transfers between devices, xor_sum(): x = x + lax.ppermute(x, axis, [(i, i ^ step) for i in range(count)])  26 us
    ppermute x17, waiting for transfers between devices, xor_sum(): x = x + lax.ppermute(x, axis, [(i, i ^ step) for i in range(count)])  24.3 us
    ppermute x3, starting transfers between devices, prepare(): lower = lax.ppermute(tail, 'chan', [(i, i + 1) for i in range(count - 1)])  8.84 us
    ppermute x3, starting transfers between devices, prepare(): upper = lax.ppermute(head, 'chan', [(i + 1, i) for i in range(count - 1)])  3.88 us
  transfers between devices with their start and end apart: 23, of which 8 were waited for; matrix products, arithmetic and copies ran while one was open for 7% of the time, Pallas kernels for 45%

profile of v3, /device:TPU:0, one launch (start us, length us, event | category | flops | bytes accessed | tf_op | source)
XLA Modules:
  0.0 161.3 jit_solution(3312273210288926499)
XLA Ops:
  0.0 1.3 slice_bitcast_fusion
  1.3 2.4 %collective-permute-start.12 = (bf16[16,8192]{1,0:T(8,128)(2,1)S(1)}, bf16[16,8192]{1,0:T(8,128)(2,1)S(1)}, u32[]{:S(2)}, u32[]{:S(2)}) collective-permute-start(bf16[16,8192]{1,0:T(8,128)(2,1)S(1)} %get-tuple-element.16), channel_id=1, source_target_pairs={{0,4},{4,8},{8,12},{12,16},{16,20},{20,24},{24,28},{1,5},{5,9},{9,... | collective-permute-start | bytes 786440 | tf_op jit(solution)/shard_map/ppermute | solution.py:229
  3.7 1.3 collective-permute-start.13
  5.0 5.1 %collective-permute-start = (bf16[16,8192]{1,0:T(8,128)(2,1)S(1)}, bf16[16,8192]{1,0:T(8,128)(2,1)S(1)}, u32[]{:S(2)}, u32[]{:S(2)}) collective-permute-start(bf16[16,8192]{1,0:T(8,128)(2,1)S(1)} %get-tuple-element.18), channel_id=1, source_target_pairs={{0,4},{4,8},{8,12},{12,16},{16,20},{20,24},{24,28},{1,5},{5,9},{9,... | collective-permute-start | bytes 786440 | tf_op jit(solution)/shard_map/ppermute | solution.py:229
  10.1 1.3 collective-permute-start.1
  13.6 1.4 select_reduce_fusion.tw_ref
  15.7 17.2 %shard_map.46.w_ref = bf16[128,8192]{1,0:T(8,128)(2,1)S(1)} custom-call(bf16[3,128,8192]{2,1,0:T(8,128)(2,1)} %rec_ref.4, bf16[16,8192]{1,0:T(8,128)(2,1)S(1)} %collective-permute-done.lo_ref, bf16[16,8192]{1,0:T(8,128)(2,1)S(1)} %collective-permute-done.1.hi_ref, bf16[128,16]{1,0:T(8,128)(2,1)S(1)} %get-tuple-element.24.blo_ref, ...), custom_call_target="tpu_custom_call" | custom-call | flops 1140850688 | bytes 4718592 | tf_op jit(solution)/shard_map/pallas_call | solution.py:170
  33.3 4.8 %collective-permute-start.2 = (bf16[4,8192]{1,0:T(4,128)(2,1)S(1)}, bf16[4,8192]{1,0:T(4,128)(2,1)S(1)}, u32[]{:S(2)}, u32[]{:S(2)}) collective-permute-start(bf16[4,8192]{1,0:T(4,128)(2,1)S(1)} %convolution_convert_fusion.2), channel_id=1, source_target_pairs={{0,4},{4,0},{8,12},{12,8},{16,20},{20,16},{24,28},{28,24},{1,5},{5... | collective-permute-start | bytes 196616 | tf_op jit(solution)/shard_map/ppermute | solution.py:203
  39.1 2.4 %collective-permute-start.3 = (bf16[4,8192]{1,0:T(4,128)(2,1)S(1)}, bf16[4,8192]{1,0:T(4,128)(2,1)S(1)}, u32[]{:S(2)}, u32[]{:S(2)}) collective-permute-start(bf16[4,8192]{1,0:T(4,128)(2,1)S(1)} %add.77), channel_id=1, source_target_pairs={{0,8},{4,12},{8,0},{12,4},{16,24},{20,28},{24,16},{28,20},{1,9},{5... | collective-permute-start | bytes 196616 | tf_op jit(solution)/shard_map/ppermute | solution.py:203
  41.5 2.6 %collective-permute-done.3 = bf16[4,8192]{1,0:T(4,128)(2,1)S(1)} collective-permute-done((bf16[4,8192]{1,0:T(4,128)(2,1)S(1)}, bf16[4,8192]{1,0:T(4,128)(2,1)S(1)}, u32[]{:S(2)}, u32[]{:S(2)}) %collective-permute-start.3) | collective-permute-done | bytes 65568 | tf_op jit(solution)/shard_map/ppermute | solution.py:203
  44.9 17.2 %shard_map.49.w_ref = bf16[128,8192]{1,0:T(8,128)(2,1)S(1)} custom-call(bf16[3,128,8192]{2,1,0:T(8,128)(2,1)} %rec_ref.4, bf16[16,8192]{1,0:T(8,128)(2,1)S(1)} %collective-permute-done.12.lo_ref, bf16[16,8192]{1,0:T(8,128)(2,1)S(1)} %collective-permute-done.13.hi_ref, bf16[128,16]{1,0:T(8,128)(2,1)S(1)} %get-tuple-element.24.blo_ref, ...), custom_call_target="tpu_custom_call" | custom-call | flops 1140850688 | bytes 4718592 | tf_op jit(solution)/shard_map/pallas_call | solution.py:170
  63.1 7.7 %shard_map.47 = f32[544,128]{1,0:T(8,128)} custom-call(bf16[128,8192]{1,0:T(8,128)(2,1)} %copy-done.2, f32[4,8320]{1,0:T(4,128)} %pad_convert_fusion.1.p_ref), custom_call_target="tpu_custom_call" | custom-call | flops 1140850688 | bytes 2506752 | tf_op jit(solution)/shard_map/pallas_call | solution.py:96
  72.9 1.3 collective-permute-start.5
  74.2 1.3 collective-permute-start.6
  75.9 2.5 %collective-permute-start.14 = (bf16[4,8192]{1,0:T(4,128)(2,1)S(1)}, bf16[4,8192]{1,0:T(4,128)(2,1)S(1)}, u32[]{:S(2)}, u32[]{:S(2)}) collective-permute-start(bf16[4,8192]{1,0:T(4,128)(2,1)S(1)} %convolution_convert_fusion), channel_id=1, source_target_pairs={{0,4},{4,0},{8,12},{12,8},{16,20},{20,16},{24,28},{28,24},{1,5},{5... | collective-permute-start | bytes 196616 | tf_op jit(solution)/shard_map/ppermute | solution.py:203
  79.3 2.0 %collective-permute-start.15 = (bf16[4,8192]{1,0:T(4,128)(2,1)S(1)}, bf16[4,8192]{1,0:T(4,128)(2,1)S(1)}, u32[]{:S(2)}, u32[]{:S(2)}) collective-permute-start(bf16[4,8192]{1,0:T(4,128)(2,1)S(1)} %add.85), channel_id=1, source_target_pairs={{0,8},{4,12},{8,0},{12,4},{16,24},{20,28},{24,16},{28,20},{1,9},{5... | collective-permute-start | bytes 196616 | tf_op jit(solution)/shard_map/ppermute | solution.py:203
  81.4 4.2 %collective-permute-done.15 = bf16[4,8192]{1,0:T(4,128)(2,1)S(1)} collective-permute-done((bf16[4,8192]{1,0:T(4,128)(2,1)S(1)}, bf16[4,8192]{1,0:T(4,128)(2,1)S(1)}, u32[]{:S(2)}, u32[]{:S(2)}) %collective-permute-start.15) | collective-permute-done | bytes 65568 | tf_op jit(solution)/shard_map/ppermute | solution.py:203
  85.6 1.8 %collective-permute-start.16 = (bf16[4,8192]{1,0:T(4,128)(2,1)S(1)}, bf16[4,8192]{1,0:T(4,128)(2,1)S(1)}, u32[]{:S(2)}, u32[]{:S(2)}) collective-permute-start(bf16[4,8192]{1,0:T(4,128)(2,1)S(1)} %add.86), channel_id=1, source_target_pairs={{0,16},{4,20},{8,24},{12,28},{16,0},{20,4},{24,8},{28,12},{1,17},{... | collective-permute-start | bytes 196616 | tf_op jit(solution)/shard_map/ppermute | solution.py:203
  87.4 1.6 collective-permute-start.10
  89.0 17.2 %shard_map.48.w_ref = bf16[128,8192]{1,0:T(8,128)(2,1)S(1)} custom-call(bf16[3,128,8192]{2,1,0:T(8,128)(2,1)} %rec_ref.4, bf16[16,8192]{1,0:T(8,128)(2,1)S(1)} %collective-permute-done.5.lo_ref, bf16[16,8192]{1,0:T(8,128)(2,1)S(1)} %collective-permute-done.6.hi_ref, bf16[128,16]{1,0:T(8,128)(2,1)S(1)} %get-tuple-element.24.blo_ref, ...), custom_call_target="tpu_custom_call" | custom-call | flops 1140850688 | bytes 4718592 | tf_op jit(solution)/shard_map/pallas_call | solution.py:170
  106.8 2.7 %collective-permute-start.11 = (f32[4,129,128]{2,0,1:T(4,128)S(1)}, f32[4,129,128]{2,0,1:T(4,128)S(1)}, u32[]{:S(2)}, u32[]{:S(2)}) collective-permute-start(f32[4,129,128]{2,0,1:T(4,128)S(1)} %add.83), channel_id=1, source_target_pairs={{0,2},{1,3},{2,0},{3,1},{4,6},{5,7},{6,4},{7,5},{8,10},{9,11},{10,... | collective-permute-start | bytes 792584 | tf_op jit(solution)/shard_map/ppermute | solution.py:203
  109.5 1.3 collective-permute-start.8
  111.5 2.3 %collective-permute-done.8 = bf16[4,8192]{1,0:T(4,128)(2,1)S(1)} collective-permute-done((bf16[4,8192]{1,0:T(4,128)(2,1)S(1)}, bf16[4,8192]{1,0:T(4,128)(2,1)S(1)}, u32[]{:S(2)}, u32[]{:S(2)}) %collective-permute-start.8) | collective-permute-done | bytes 65568 | tf_op jit(solution)/shard_map/ppermute | solution.py:203
  114.2 7.7 %shard_map.50 = f32[544,128]{1,0:T(8,128)} custom-call(bf16[128,8192]{1,0:T(8,128)(2,1)} %copy-done.1, f32[4,8320]{1,0:T(4,128)} %pad_convert_fusion.p_ref), custom_call_target="tpu_custom_call" | custom-call | flops 1140850688 | bytes 2506752 | tf_op jit(solution)/shard_map/pallas_call | solution.py:96
  124.6 6.7 %shard_map.51 = f32[272,128]{1,0:T(8,128)} custom-call(bf16[128,8192]{1,0:T(8,128)(2,1)} %copy-done, f32[2,8320]{1,0:T(2,128)} %get-tuple-element.26.p_ref), custom_call_target="tpu_custom_call" | custom-call | flops 570425344 | bytes 2301952 | tf_op jit(solution)/shard_map/pallas_call | solution.py:96
  132.3 1.6 %collective-permute-start.19 = (f32[2,129,128]{2,0,1:T(2,128)S(1)}, f32[2,129,128]{2,0,1:T(2,128)S(1)}, u32[]{:S(2)}, u32[]{:S(2)}) collective-permute-start(f32[2,129,128]{2,0,1:T(2,128)S(1)} %copy.16), channel_id=1, source_target_pairs={{0,1},{1,0},{2,3},{3,2},{4,5},{5,4},{6,7},{7,6},{8,9},{9,8},{10,11... | collective-permute-start | bytes 396296 | tf_op jit(solution)/shard_map/ppermute | solution.py:203
  135.1 6.7 %shard_map.52 = f32[272,128]{1,0:T(8,128)} custom-call(bf16[128,8192]{1,0:T(8,128)(2,1)} %copy-done, f32[2,8320]{1,0:T(2,128)} %get-tuple-element.25.p_ref), custom_call_target="tpu_custom_call" | custom-call | flops 570425344 | bytes 2301952 | tf_op jit(solution)/shard_map/pallas_call | solution.py:96
  143.4 2.0 %collective-permute-start.20 = (f32[2,129,128]{2,0,1:T(2,128)S(1)}, f32[2,129,128]{2,0,1:T(2,128)S(1)}, u32[]{:S(2)}, u32[]{:S(2)}) collective-permute-start(f32[2,129,128]{2,0,1:T(2,128)S(1)} %copy_add_fusion.1), channel_id=1, source_target_pairs={{0,2},{1,3},{2,0},{3,1},{4,6},{5,7},{6,4},{7,5},{8,10},{9,11},{10,... | collective-permute-start | bytes 396296 | tf_op jit(solution)/shard_map/ppermute | solution.py:203
  145.4 5.4 %collective-permute-done.21 = f32[2,129,128]{2,0,1:T(2,128)S(1)} collective-permute-done((f32[2,129,128]{2,0,1:T(2,128)S(1)}, f32[2,129,128]{2,0,1:T(2,128)S(1)}, u32[]{:S(2)}, u32[]{:S(2)}) %collective-permute-start.21) | collective-permute-done | bytes 132128 | tf_op jit(solution)/shard_map/ppermute | solution.py:203
  151.9 1.1 collective-permute-done.20
  153.1 6.8 %collective-permute-done.22 = f32[2,129,128]{2,0,1:T(2,128)S(1)} collective-permute-done((f32[2,129,128]{2,0,1:T(2,128)S(1)}, f32[2,129,128]{2,0,1:T(2,128)S(1)}, u32[]{:S(2)}, u32[]{:S(2)}) %collective-permute-start.22) | collective-permute-done | bytes 132128 | tf_op jit(solution)/shard_map/ppermute | solution.py:203
  160.2 1.1 maximum_multiply_fusion
  (75 shorter events, 18.9 us)
Async XLA Ops:
  1.3 43.6 %collective-permute-start.12 = (bf16[16,8192]{1,0:T(8,128)(2,1)S(1)}, bf16[16,8192]{1,0:T(8,128)(2,1)S(1)}, u32[]{:S(2)}, u32[]{:S(2)}) collective-permute-start(bf16[16,8192]{1,0:T(8,128)(2,1)S(1)} %get-tuple-element.16), channel_id=1, source_target_pairs={{0,4},{4,8},{8,12},{12,16},{16,20},{20,24},{24,28},{1,5},{5,9},{9,... | collective-permute-start | bytes 786440 | tf_op jit(solution)/shard_map/ppermute | solution.py:229
  3.7 41.2 %collective-permute-start.13 = (bf16[16,8192]{1,0:T(8,128)(2,1)S(1)}, bf16[16,8192]{1,0:T(8,128)(2,1)S(1)}, u32[]{:S(2)}, u32[]{:S(2)}) collective-permute-start(bf16[16,8192]{1,0:T(8,128)(2,1)S(1)} %get-tuple-element.15), channel_id=1, source_target_pairs={{4,0},{8,4},{12,8},{16,12},{20,16},{24,20},{28,24},{5,1},{9,5},{13... | collective-permute-start | bytes 786440 | tf_op jit(solution)/shard_map/ppermute | solution.py:230
  5.0 10.7 %collective-permute-start = (bf16[16,8192]{1,0:T(8,128)(2,1)S(1)}, bf16[16,8192]{1,0:T(8,128)(2,1)S(1)}, u32[]{:S(2)}, u32[]{:S(2)}) collective-permute-start(bf16[16,8192]{1,0:T(8,128)(2,1)S(1)} %get-tuple-element.18), channel_id=1, source_target_pairs={{0,4},{4,8},{8,12},{12,16},{16,20},{20,24},{24,28},{1,5},{5,9},{9,... | collective-permute-start | bytes 786440 | tf_op jit(solution)/shard_map/ppermute | solution.py:229
  10.1 5.6 %collective-permute-start.1 = (bf16[16,8192]{1,0:T(8,128)(2,1)S(1)}, bf16[16,8192]{1,0:T(8,128)(2,1)S(1)}, u32[]{:S(2)}, u32[]{:S(2)}) collective-permute-start(bf16[16,8192]{1,0:T(8,128)(2,1)S(1)} %get-tuple-element.17), channel_id=1, source_target_pairs={{4,0},{8,4},{12,8},{16,12},{20,16},{24,20},{28,24},{5,1},{9,5},{13... | collective-permute-start | bytes 786440 | tf_op jit(solution)/shard_map/ppermute | solution.py:230
  32.9 29.2 %copy-start.2 = (bf16[128,8192]{1,0:T(8,128)(2,1)}, bf16[128,8192]{1,0:T(8,128)(2,1)S(1)}, u32[]{:S(2)}) copy-start(bf16[128,8192]{1,0:T(8,128)(2,1)S(1)} %shard_map.46.w_ref) | copy-start | bytes 6291460
  33.3 5.7 %collective-permute-start.2 = (bf16[4,8192]{1,0:T(4,128)(2,1)S(1)}, bf16[4,8192]{1,0:T(4,128)(2,1)S(1)}, u32[]{:S(2)}, u32[]{:S(2)}) collective-permute-start(bf16[4,8192]{1,0:T(4,128)(2,1)S(1)} %convolution_convert_fusion.2), channel_id=1, source_target_pairs={{0,4},{4,0},{8,12},{12,8},{16,20},{20,16},{24,28},{28,24},{1,5},{5... | collective-permute-start | bytes 196616 | tf_op jit(solution)/shard_map/ppermute | solution.py:203
  39.1 5.0 %collective-permute-start.3 = (bf16[4,8192]{1,0:T(4,128)(2,1)S(1)}, bf16[4,8192]{1,0:T(4,128)(2,1)S(1)}, u32[]{:S(2)}, u32[]{:S(2)}) collective-permute-start(bf16[4,8192]{1,0:T(4,128)(2,1)S(1)} %add.77), channel_id=1, source_target_pairs={{0,8},{4,12},{8,0},{12,4},{16,24},{20,28},{24,16},{28,20},{1,9},{5... | collective-permute-start | bytes 196616 | tf_op jit(solution)/shard_map/ppermute | solution.py:203
  44.1 18.0 %collective-permute-start.4 = (bf16[4,8192]{1,0:T(4,128)(2,1)S(1)}, bf16[4,8192]{1,0:T(4,128)(2,1)S(1)}, u32[]{:S(2)}, u32[]{:S(2)}) collective-permute-start(bf16[4,8192]{1,0:T(4,128)(2,1)S(1)} %add.78), channel_id=1, source_target_pairs={{0,16},{4,20},{8,24},{12,28},{16,0},{20,4},{24,8},{28,12},{1,17},{... | collective-permute-start | bytes 196616 | tf_op jit(solution)/shard_map/ppermute | solution.py:203
  62.1 13.4 %copy-start.1 = (bf16[128,8192]{1,0:T(8,128)(2,1)}, bf16[128,8192]{1,0:T(8,128)(2,1)S(1)}, u32[]{:S(2)}) copy-start(bf16[128,8192]{1,0:T(8,128)(2,1)S(1)} %shard_map.49.w_ref) | copy-start | bytes 6291460
  72.9 16.1 %collective-permute-start.5 = (bf16[16,8192]{1,0:T(8,128)(2,1)S(1)}, bf16[16,8192]{1,0:T(8,128)(2,1)S(1)}, u32[]{:S(2)}, u32[]{:S(2)}) collective-permute-start(bf16[16,8192]{1,0:T(8,128)(2,1)S(1)} %get-tuple-element.20), channel_id=1, source_target_pairs={{0,4},{4,8},{8,12},{12,16},{16,20},{20,24},{24,28},{1,5},{5,9},{9,... | collective-permute-start | bytes 786440 | tf_op jit(solution)/shard_map/ppermute | solution.py:229
  74.2 14.8 %collective-permute-start.6 = (bf16[16,8192]{1,0:T(8,128)(2,1)S(1)}, bf16[16,8192]{1,0:T(8,128)(2,1)S(1)}, u32[]{:S(2)}, u32[]{:S(2)}) collective-permute-start(bf16[16,8192]{1,0:T(8,128)(2,1)S(1)} %get-tuple-element.19), channel_id=1, source_target_pairs={{4,0},{8,4},{12,8},{16,12},{20,16},{24,20},{28,24},{5,1},{9,5},{13... | collective-permute-start | bytes 786440 | tf_op jit(solution)/shard_map/ppermute | solution.py:230
  75.9 3.4 %collective-permute-start.14 = (bf16[4,8192]{1,0:T(4,128)(2,1)S(1)}, bf16[4,8192]{1,0:T(4,128)(2,1)S(1)}, u32[]{:S(2)}, u32[]{:S(2)}) collective-permute-start(bf16[4,8192]{1,0:T(4,128)(2,1)S(1)} %convolution_convert_fusion), channel_id=1, source_target_pairs={{0,4},{4,0},{8,12},{12,8},{16,20},{20,16},{24,28},{28,24},{1,5},{5... | collective-permute-start | bytes 196616 | tf_op jit(solution)/shard_map/ppermute | solution.py:203
  79.3 6.3 %collective-permute-start.15 = (bf16[4,8192]{1,0:T(4,128)(2,1)S(1)}, bf16[4,8192]{1,0:T(4,128)(2,1)S(1)}, u32[]{:S(2)}, u32[]{:S(2)}) collective-permute-start(bf16[4,8192]{1,0:T(4,128)(2,1)S(1)} %add.85), channel_id=1, source_target_pairs={{0,8},{4,12},{8,0},{12,4},{16,24},{20,28},{24,16},{28,20},{1,9},{5... | collective-permute-start | bytes 196616 | tf_op jit(solution)/shard_map/ppermute | solution.py:203
  85.6 21.0 %collective-permute-start.16 = (bf16[4,8192]{1,0:T(4,128)(2,1)S(1)}, bf16[4,8192]{1,0:T(4,128)(2,1)S(1)}, u32[]{:S(2)}, u32[]{:S(2)}) collective-permute-start(bf16[4,8192]{1,0:T(4,128)(2,1)S(1)} %add.86), channel_id=1, source_target_pairs={{0,16},{4,20},{8,24},{12,28},{16,0},{20,4},{24,8},{28,12},{1,17},{... | collective-permute-start | bytes 196616 | tf_op jit(solution)/shard_map/ppermute | solution.py:203
  87.4 19.3 %collective-permute-start.10 = (f32[4,129,128]{2,0,1:T(4,128)S(1)}, f32[4,129,128]{2,0,1:T(4,128)S(1)}, u32[]{:S(2)}, u32[]{:S(2)}) collective-permute-start(f32[4,129,128]{2,0,1:T(4,128)S(1)} %copy.14), channel_id=1, source_target_pairs={{0,1},{1,0},{2,3},{3,2},{4,5},{5,4},{6,7},{7,6},{8,9},{9,8},{10,11... | collective-permute-start | bytes 792584 | tf_op jit(solution)/shard_map/ppermute | solution.py:203
  106.2 15.8 %copy-start = (bf16[128,8192]{1,0:T(8,128)(2,1)}, bf16[128,8192]{1,0:T(8,128)(2,1)S(1)}, u32[]{:S(2)}) copy-start(bf16[128,8192]{1,0:T(8,128)(2,1)S(1)} %shard_map.48.w_ref) | copy-start | bytes 6291460
  106.6 2.9 %collective-permute-start.7 = (bf16[4,8192]{1,0:T(4,128)(2,1)S(1)}, bf16[4,8192]{1,0:T(4,128)(2,1)S(1)}, u32[]{:S(2)}, u32[]{:S(2)}) collective-permute-start(bf16[4,8192]{1,0:T(4,128)(2,1)S(1)} %convolution_convert_fusion.1), channel_id=1, source_target_pairs={{0,4},{4,0},{8,12},{12,8},{16,20},{20,16},{24,28},{28,24},{1,5},{5... | collective-permute-start | bytes 196616 | tf_op jit(solution)/shard_map/ppermute | solution.py:203
  106.8 16.9 %collective-permute-start.11 = (f32[4,129,128]{2,0,1:T(4,128)S(1)}, f32[4,129,128]{2,0,1:T(4,128)S(1)}, u32[]{:S(2)}, u32[]{:S(2)}) collective-permute-start(f32[4,129,128]{2,0,1:T(4,128)S(1)} %add.83), channel_id=1, source_target_pairs={{0,2},{1,3},{2,0},{3,1},{4,6},{5,7},{6,4},{7,5},{8,10},{9,11},{10,... | collective-permute-start | bytes 792584 | tf_op jit(solution)/shard_map/ppermute | solution.py:203
  109.5 4.3 %collective-permute-start.8 = (bf16[4,8192]{1,0:T(4,128)(2,1)S(1)}, bf16[4,8192]{1,0:T(4,128)(2,1)S(1)}, u32[]{:S(2)}, u32[]{:S(2)}) collective-permute-start(bf16[4,8192]{1,0:T(4,128)(2,1)S(1)} %add.80), channel_id=1, source_target_pairs={{0,8},{4,12},{8,0},{12,4},{16,24},{20,28},{24,16},{28,20},{1,9},{5... | collective-permute-start | bytes 196616 | tf_op jit(solution)/shard_map/ppermute | solution.py:203
  113.8 9.7 %collective-permute-start.9 = (bf16[4,8192]{1,0:T(4,128)(2,1)S(1)}, bf16[4,8192]{1,0:T(4,128)(2,1)S(1)}, u32[]{:S(2)}, u32[]{:S(2)}) collective-permute-start(bf16[4,8192]{1,0:T(4,128)(2,1)S(1)} %add.81), channel_id=1, source_target_pairs={{0,16},{4,20},{8,24},{12,28},{16,0},{20,4},{24,8},{28,12},{1,17},{... | collective-permute-start | bytes 196616 | tf_op jit(solution)/shard_map/ppermute | solution.py:203
  122.0 12.0 %copy-start.4 = (f32[544,128]{1,0:T(8,128)S(1)}, f32[544,128]{1,0:T(8,128)}, u32[]{:S(2)}) copy-start(f32[544,128]{1,0:T(8,128)} %shard_map.50) | copy-start | bytes 835588
  123.1 10.9 %collective-permute-start.17 = (f32[4,129,128]{2,0,1:T(4,128)S(1)}, f32[4,129,128]{2,0,1:T(4,128)S(1)}, u32[]{:S(2)}, u32[]{:S(2)}) collective-permute-start(f32[4,129,128]{2,0,1:T(4,128)S(1)} %copy.15), channel_id=1, source_target_pairs={{0,1},{1,0},{2,3},{3,2},{4,5},{5,4},{6,7},{7,6},{8,9},{9,8},{10,11... | collective-permute-start | bytes 792584 | tf_op jit(solution)/shard_map/ppermute | solution.py:203
  131.2 12.1 %copy-start.3 = (f32[272,128]{1,0:T(8,128)S(1)}, f32[272,128]{1,0:T(8,128)}, u32[]{:S(2)}) copy-start(f32[272,128]{1,0:T(8,128)} %shard_map.51) | copy-start | bytes 417796
  132.3 11.0 %collective-permute-start.19 = (f32[2,129,128]{2,0,1:T(2,128)S(1)}, f32[2,129,128]{2,0,1:T(2,128)S(1)}, u32[]{:S(2)}, u32[]{:S(2)}) collective-permute-start(f32[2,129,128]{2,0,1:T(2,128)S(1)} %copy.16), channel_id=1, source_target_pairs={{0,1},{1,0},{2,3},{3,2},{4,5},{5,4},{6,7},{7,6},{8,9},{9,8},{10,11... | collective-permute-start | bytes 396296 | tf_op jit(solution)/shard_map/ppermute | solution.py:203
  134.0 17.8 %collective-permute-start.18 = (f32[4,129,128]{2,0,1:T(4,128)S(1)}, f32[4,129,128]{2,0,1:T(4,128)S(1)}, u32[]{:S(2)}, u32[]{:S(2)}) collective-permute-start(f32[4,129,128]{2,0,1:T(4,128)S(1)} %copy_add_fusion), channel_id=1, source_target_pairs={{0,2},{1,3},{2,0},{3,1},{4,6},{5,7},{6,4},{7,5},{8,10},{9,11},{10,... | collective-permute-start | bytes 792584 | tf_op jit(solution)/shard_map/ppermute | solution.py:203
  142.8 7.9 %collective-permute-start.21 = (f32[2,129,128]{2,0,1:T(2,128)S(1)}, f32[2,129,128]{2,0,1:T(2,128)S(1)}, u32[]{:S(2)}, u32[]{:S(2)}) collective-permute-start(f32[2,129,128]{2,0,1:T(2,128)S(1)} %copy.17), channel_id=1, source_target_pairs={{0,1},{1,0},{2,3},{3,2},{4,5},{5,4},{6,7},{7,6},{8,9},{9,8},{10,11... | collective-permute-start | bytes 396296 | tf_op jit(solution)/shard_map/ppermute | solution.py:203
  143.4 9.6 %collective-permute-start.20 = (f32[2,129,128]{2,0,1:T(2,128)S(1)}, f32[2,129,128]{2,0,1:T(2,128)S(1)}, u32[]{:S(2)}, u32[]{:S(2)}) collective-permute-start(f32[2,129,128]{2,0,1:T(2,128)S(1)} %copy_add_fusion.1), channel_id=1, source_target_pairs={{0,2},{1,3},{2,0},{3,1},{4,6},{5,7},{6,4},{7,5},{8,10},{9,11},{10,... | collective-permute-start | bytes 396296 | tf_op jit(solution)/shard_map/ppermute | solution.py:203
  151.8 8.2 %collective-permute-start.22 = (f32[2,129,128]{2,0,1:T(2,128)S(1)}, f32[2,129,128]{2,0,1:T(2,128)S(1)}, u32[]{:S(2)}, u32[]{:S(2)}) collective-permute-start(f32[2,129,128]{2,0,1:T(2,128)S(1)} %copy_add_fusion.2), channel_id=1, source_target_pairs={{0,2},{1,3},{2,0},{3,1},{4,6},{5,7},{6,4},{7,5},{8,10},{9,11},{10,... | collective-permute-start | bytes 396296 | tf_op jit(solution)/shard_map/ppermute | solution.py:203
